TPU v7x, 32 devices: a whole 2x2x4 slice. The times are simulated.
32 devices in a mesh: gx: 16 (over z, y, x), gy: 2 (over core).
Axes of the slice: x: 2, y: 2, z: 4, core: 2. Of those that a mesh axis runs over, the one named last changes fastest.
Arguments:
- load_parts: bfloat16 [16, 2, 4, 192, 384], P('gx', 'gy'), may hold values from -6 to 6
- schur: bfloat16 [16, 2, 4, 384, 384], P('gx', 'gy'), may hold values from -4 to 4
- deluxe: bfloat16 [16, 2, 4, 384, 384], P('gx', 'gy'), may hold values from -4 to 4
- panels: bfloat16 [16, 2, 4, 384, 384], P('gx', 'gy'), may hold values from -4 to 4
- coarse_inverse: float32 [128, 128], P(('gx', 'gy')), may hold values from -1 to 1
- primal_dofs: int32 [16, 2, 4], P('gx', 'gy'), may hold values from 0 to 1535
- damage_flags: int32 [16, 2, 4], P('gx', 'gy'), may hold values 0 or 1
Outputs:
- increment: bfloat16 [16, 2, 4, 192, 384], P('gx', 'gy')
Inputs may be any that keep to these rules, and one draw needn't show every extreme that they name: `primal_dofs`: each entry names a face times 384 plus a position on that face.
All inputs are finite; a program needn't handle non-finite values. No bound on the sum of `damage_flags` on one device may be relied on, other than what follows from the above.
Results may differ from a plain program's by a relative error of at most 0.003.
The roundings to bfloat16 on the way count: a program that leaves them out, or rounds other values in their place, can miss the bound.
Values may be sent and summed in bfloat16 or wider, within the bound.
No kernel may reach another device: no remote copies, remote signals or barrier semaphores. Data moves between devices by JAX's collectives and lax.ppermute only.
A program may use at most 64 MiB of HBM per device.

v0:
```python
import jax
import jax.numpy as jnp
from jax import lax
from jax.sharding import PartitionSpec as P


def with_halo(block, sides, width):
    for axis, dim in sides:
        count = lax.axis_size(axis)
        forward = [(i, i + 1) for i in range(count - 1)]
        backward = [(target, source) for source, target in forward]
        low = lax.ppermute(
            lax.slice_in_dim(block, block.shape[dim] - width, None, axis=dim), axis, forward
        )
        high = lax.ppermute(lax.slice_in_dim(block, 0, width, axis=dim), axis, backward)
        block = jnp.concatenate([low, block, high], axis=dim)
    return block


def face_mul(vectors, matrices):
    return jnp.einsum("fry,fyx->frx", vectors, matrices, preferred_element_type=jnp.float32)


def face_mul_turned(vectors, matrices):
    return jnp.einsum("fry,fxy->frx", vectors, matrices, preferred_element_type=jnp.float32)


def face_pairs(values):
    along_first = with_halo(values[0:2], (("gx", 0),), 1)
    along_second = with_halo(values[2:4], (("gy", 0),), 1)
    return jnp.stack([along_first[0], along_first[3], along_second[0], along_second[3]], axis=0)


def image_pairs(values):
    along_first = with_halo(values[0:2], (("gx", 0),), 1)
    along_second = with_halo(values[2:4], (("gy", 0),), 1)
    return jnp.stack([along_first[0], along_first[3], along_second[0], along_second[3]], axis=0)


def per_device(load_parts, schur, deluxe, panels, coarse_inverse, primal_dofs, damage_flags):
    loads_here = load_parts[0, 0]
    schur_panel = schur[0, 0]
    deluxe_panel = deluxe[0, 0]
    inverse_panel = panels[0, 0]
    primal_slots = primal_dofs[0, 0]
    flag_values = damage_flags[0, 0]
    width = loads_here.shape[2]
    primal_count = primal_slots.shape[0]
    positions = jnp.arange(4 * width, dtype=jnp.int32)
    picks = (primal_slots[:, None] == positions[None, :]).reshape(primal_count, 4, width)
    picks_half = picks.astype(jnp.bfloat16)
    picks_full = picks.astype(jnp.float32)
    flags_full = flag_values.astype(jnp.float32)

    def add_coarse(piece):
        return jnp.dot(coarse_inverse, piece.astype(jnp.float32), precision=lax.Precision.HIGHEST)

    def precondition(resid):
        scaled = face_mul_turned(resid.astype(jnp.bfloat16), deluxe_panel).astype(jnp.bfloat16)
        local_part = face_mul(scaled, inverse_panel)
        extra = face_mul(local_part.astype(jnp.bfloat16), inverse_panel)
        softened = local_part + 0.5 * flags_full[:, None, None] * extra
        primal = jnp.einsum(
            "kfx,frx->kr", picks_half, scaled, preferred_element_type=jnp.float32
        ).astype(jnp.bfloat16)
        coarse = add_coarse(lax.all_gather(primal, ("gx", "gy"), axis=0, tiled=True))
        placed = jnp.einsum("kfx,kr->frx", picks_full, coarse, precision=lax.Precision.HIGHEST)
        weighted = (softened + placed).astype(jnp.bfloat16)
        spread = face_mul(weighted, deluxe_panel).astype(jnp.bfloat16)
        return spread.astype(jnp.float32) + face_pairs(spread).astype(jnp.float32)

    def apply_operator(field):
        bent = face_mul(field.astype(jnp.bfloat16), schur_panel).astype(jnp.bfloat16)
        return bent.astype(jnp.float32) + image_pairs(bent).astype(jnp.float32)

    resid0 = loads_here.astype(jnp.float32) + face_pairs(loads_here).astype(jnp.float32)
    first = precondition(resid0)
    resid1 = resid0 - apply_operator(first)
    second = precondition(resid1)
    top = lax.psum(jnp.sum(resid1 * second, axis=(0, 2)), ("gx", "gy"))
    curved = apply_operator(second)
    bottom = lax.psum(jnp.sum(second * curved, axis=(0, 2)), ("gx", "gy"))
    step_len = top / bottom
    result = (first + step_len[:, None] * second).astype(jnp.bfloat16)
    return result[None, None]


def solution(mesh):
    return jax.shard_map(
        per_device,
        mesh=mesh,
        in_specs=(
            P("gx", "gy", None, None, None),
            P("gx", "gy", None, None, None),
            P("gx", "gy", None, None, None),
            P("gx", "gy", None, None, None),
            P(("gx", "gy"), None),
            P("gx", "gy", None),
            P("gx", "gy", None),
        ),
        out_specs=P("gx", "gy", None, None, None),
        check_vma=False,
    )
```

profile of v0, /device:TPU:10, one launch (start us, length us, event | category | flops | bytes accessed | tf_op | source)
XLA Modules:
  0.0 210.2 jit_solution(9755467577524988544)
XLA Ops:
  0.0 1.3 slice_bitcast_fusion.3
  1.3 3.4 %collective-permute-start = (bf16[1,192,384]{2,1,0:T(8,128)(2,1)S(1)}, bf16[1,192,384]{2,1,0:T(8,128)(2,1)S(1)}, u32[]{:S(2)}, u32[]{:S(2)}) collective-permute-start(bf16[1,192,384]{2,1,0:T(8,128)(2,1)S(1)} %get-tuple-element.23), channel_id=1, source_target_pairs={{0,2},{2,4},{4,6},{6,8},{8,10},{10,12},{12,14},{14,16},{16,18},{18... | collective-permute-start | bytes 442376 | tf_op jit(solution)/shard_map/ppermute | solution.py:12
  4.7 2.4 %collective-permute-start.1 = (bf16[1,192,384]{2,1,0:T(8,128)(2,1)S(1)}, bf16[1,192,384]{2,1,0:T(8,128)(2,1)S(1)}, u32[]{:S(2)}, u32[]{:S(2)}) collective-permute-start(bf16[1,192,384]{2,1,0:T(8,128)(2,1)S(1)} %get-tuple-element.24), channel_id=1, source_target_pairs={{2,0},{4,2},{6,4},{8,6},{10,8},{12,10},{14,12},{16,14},{18,16},{20... | collective-permute-start | bytes 442376 | tf_op jit(solution)/shard_map/ppermute | solution.py:15
  7.2 1.3 collective-permute-start.3
  8.5 3.0 %collective-permute-start.2 = (bf16[1,192,384]{2,1,0:T(8,128)(2,1)S(1)}, bf16[1,192,384]{2,1,0:T(8,128)(2,1)S(1)}, u32[]{:S(2)}, u32[]{:S(2)}) collective-permute-start(bf16[1,192,384]{2,1,0:T(8,128)(2,1)S(1)} %get-tuple-element.26), channel_id=1, source_target_pairs={{0,1},{2,3},{4,5},{6,7},{8,9},{10,11},{12,13},{14,15},{16,17},{18,... | collective-permute-start | bytes 442376 | tf_op jit(solution)/shard_map/ppermute | solution.py:12
  11.6 0.6 multiply_bitcast_fusion
  12.2 0.8 collective-permute-done.1
  13.0 0.6 convolution_convert_fusion.5
  13.7 0.3 fusion.25
  14.0 34.1 %all-gather = bf16[32,4,192]{2,1,0:T(4,128)(2,1)} all-gather(bf16[1,4,192]{2,1,0:T(4,128)(2,1)S(1)} %fusion.25), channel_id=1, replica_groups=mesh['gx'=16,'gy'=2] {'gx','gy'}, dimensions={0}, use_global_device_ids=true | all-gather | bytes 50688 | tf_op jit(solution)/shard_map/all_gather | solution.py:66
  48.0 1.5 reshape.37
  49.6 1.5 fusion.14
  51.1 0.1 convolution_bitcast_fusion.5
  51.2 1.8 convolution_bitcast_fusion.1
  53.0 2.9 %convolution_convert_fusion.4 = bf16[4,192,384]{2,1,0:T(8,128)(2,1)S(1)} fusion(f32[4,192,384]{2,1,0:T(8,128)} %convolution_bitcast_fusion.1, f32[4,192,384]{2,1,0:T(8,128)} %fusion.14, bf16[1,1,4,384,384]{4,3,2,1,0:T(8,128)(2,1)S(1)} %copy-done.1, bf16[1,1,4,384,384]{4,3,2,1,0:T(8,128)(2,1)S(1)} %copy-done, f32[4]{0:T(128)} %multiply_bitcast_fusion), kind=kOutput, calls=%fused_computation.14 | convolution fusion | flops 454754304 | bytes 5308432 | tf_op jit(solution)/shard_map/fry,fyx->frx/dot_general | solution.py:21
  56.0 3.5 %collective-permute-start.4 = (bf16[1,192,384]{2,1,0:T(8,128)(2,1)S(1)}, bf16[1,192,384]{2,1,0:T(8,128)(2,1)S(1)}, u32[]{:S(2)}, u32[]{:S(2)}) collective-permute-start(bf16[1,192,384]{2,1,0:T(8,128)(2,1)S(1)} %get-tuple-element.19), channel_id=1, source_target_pairs={{0,2},{2,4},{4,6},{6,8},{8,10},{10,12},{12,14},{14,16},{16,18},{18... | collective-permute-start | bytes 442376 | tf_op jit(solution)/shard_map/ppermute | solution.py:12
  59.5 1.3 collective-permute-start.7
  60.8 3.0 %collective-permute-start.6 = (bf16[1,192,384]{2,1,0:T(8,128)(2,1)S(1)}, bf16[1,192,384]{2,1,0:T(8,128)(2,1)S(1)}, u32[]{:S(2)}, u32[]{:S(2)}) collective-permute-start(bf16[1,192,384]{2,1,0:T(8,128)(2,1)S(1)} %get-tuple-element.21), channel_id=1, source_target_pairs={{0,1},{2,3},{4,5},{6,7},{8,9},{10,11},{12,13},{14,15},{16,17},{18,... | collective-permute-start | bytes 442376 | tf_op jit(solution)/shard_map/ppermute | solution.py:12
  63.9 4.6 %collective-permute-start.5 = (bf16[1,192,384]{2,1,0:T(8,128)(2,1)S(1)}, bf16[1,192,384]{2,1,0:T(8,128)(2,1)S(1)}, u32[]{:S(2)}, u32[]{:S(2)}) collective-permute-start(bf16[1,192,384]{2,1,0:T(8,128)(2,1)S(1)} %get-tuple-element.22), channel_id=1, source_target_pairs={{2,0},{4,2},{6,4},{8,6},{10,8},{12,10},{14,12},{16,14},{18,16},{20... | collective-permute-start | bytes 442376 | tf_op jit(solution)/shard_map/ppermute | solution.py:15
  68.6 3.3 %collective-permute-done.5 = bf16[1,192,384]{2,1,0:T(8,128)(2,1)S(1)} collective-permute-done((bf16[1,192,384]{2,1,0:T(8,128)(2,1)S(1)}, bf16[1,192,384]{2,1,0:T(8,128)(2,1)S(1)}, u32[]{:S(2)}, u32[]{:S(2)}) %collective-permute-start.5) | collective-permute-done | bytes 147488 | tf_op jit(solution)/shard_map/ppermute | solution.py:15
  71.8 0.5 convolution_convert_fusion.3
  72.6 3.5 %collective-permute-start.8 = (bf16[1,192,384]{2,1,0:T(8,128)(2,1)S(1)}, bf16[1,192,384]{2,1,0:T(8,128)(2,1)S(1)}, u32[]{:S(2)}, u32[]{:S(2)}) collective-permute-start(bf16[1,192,384]{2,1,0:T(8,128)(2,1)S(1)} %get-tuple-element.15), channel_id=1, source_target_pairs={{0,2},{2,4},{4,6},{6,8},{8,10},{10,12},{12,14},{14,16},{16,18},{18... | collective-permute-start | bytes 442376 | tf_op jit(solution)/shard_map/ppermute | solution.py:12
  76.1 1.3 collective-permute-start.11
  77.4 3.0 %collective-permute-start.10 = (bf16[1,192,384]{2,1,0:T(8,128)(2,1)S(1)}, bf16[1,192,384]{2,1,0:T(8,128)(2,1)S(1)}, u32[]{:S(2)}, u32[]{:S(2)}) collective-permute-start(bf16[1,192,384]{2,1,0:T(8,128)(2,1)S(1)} %get-tuple-element.17), channel_id=1, source_target_pairs={{0,1},{2,3},{4,5},{6,7},{8,9},{10,11},{12,13},{14,15},{16,17},{18,... | collective-permute-start | bytes 442376 | tf_op jit(solution)/shard_map/ppermute | solution.py:12
  80.4 3.6 %collective-permute-start.9 = (bf16[1,192,384]{2,1,0:T(8,128)(2,1)S(1)}, bf16[1,192,384]{2,1,0:T(8,128)(2,1)S(1)}, u32[]{:S(2)}, u32[]{:S(2)}) collective-permute-start(bf16[1,192,384]{2,1,0:T(8,128)(2,1)S(1)} %get-tuple-element.18), channel_id=1, source_target_pairs={{2,0},{4,2},{6,4},{8,6},{10,8},{12,10},{14,12},{16,14},{18,16},{20... | collective-permute-start | bytes 442376 | tf_op jit(solution)/shard_map/ppermute | solution.py:15
  84.1 5.0 %collective-permute-done.9 = bf16[1,192,384]{2,1,0:T(8,128)(2,1)S(1)} collective-permute-done((bf16[1,192,384]{2,1,0:T(8,128)(2,1)S(1)}, bf16[1,192,384]{2,1,0:T(8,128)(2,1)S(1)}, u32[]{:S(2)}, u32[]{:S(2)}) %collective-permute-start.9) | collective-permute-done | bytes 147488 | tf_op jit(solution)/shard_map/ppermute | solution.py:15
  89.2 0.7 convolution_convert_fusion.2
  89.9 0.3 fusion.24
  90.2 1.6 fusion.10
  91.7 35.3 %all-gather.1 = bf16[32,4,192]{2,1,0:T(4,128)(2,1)S(1)} all-gather(bf16[1,4,192]{2,1,0:T(4,128)(2,1)S(1)} %fusion.24), channel_id=1, replica_groups=mesh['gx'=16,'gy'=2] {'gx','gy'}, dimensions={0}, use_global_device_ids=true | all-gather | bytes 50688 | tf_op jit(solution)/shard_map/all_gather | solution.py:66
  127.1 0.1 convolution_bitcast_fusion.4
  127.2 1.8 convolution_bitcast_fusion
  129.0 2.9 %convolution_convert_fusion.1 = bf16[4,192,384]{2,1,0:T(8,128)(2,1)S(1)} fusion(f32[4,192,384]{2,1,0:T(8,128)} %convolution_bitcast_fusion, f32[4,192,384]{2,1,0:T(8,128)} %fusion.10, bf16[1,1,4,384,384]{4,3,2,1,0:T(8,128)(2,1)S(1)} %copy-done.1, bf16[1,1,4,384,384]{4,3,2,1,0:T(8,128)(2,1)S(1)} %copy-done, f32[4]{0:T(128)} %multiply_bitcast_fusion), kind=kOutput, calls=%fused_computation.11 | convolution fusion | flops 454754304 | bytes 5308432 | tf_op jit(solution)/shard_map/fry,fyx->frx/dot_general | solution.py:21
  132.0 2.1 collective-permute-start.12
  134.1 1.3 collective-permute-start.15
  135.4 3.0 %collective-permute-start.14 = (bf16[1,192,384]{2,1,0:T(8,128)(2,1)S(1)}, bf16[1,192,384]{2,1,0:T(8,128)(2,1)S(1)}, u32[]{:S(2)}, u32[]{:S(2)}) collective-permute-start(bf16[1,192,384]{2,1,0:T(8,128)(2,1)S(1)} %get-tuple-element.13), channel_id=1, source_target_pairs={{0,1},{2,3},{4,5},{6,7},{8,9},{10,11},{12,13},{14,15},{16,17},{18,... | collective-permute-start | bytes 442376 | tf_op jit(solution)/shard_map/ppermute | solution.py:12
  138.4 3.9 %collective-permute-start.13 = (bf16[1,192,384]{2,1,0:T(8,128)(2,1)S(1)}, bf16[1,192,384]{2,1,0:T(8,128)(2,1)S(1)}, u32[]{:S(2)}, u32[]{:S(2)}) collective-permute-start(bf16[1,192,384]{2,1,0:T(8,128)(2,1)S(1)} %get-tuple-element.14), channel_id=1, source_target_pairs={{2,0},{4,2},{6,4},{8,6},{10,8},{12,10},{14,12},{16,14},{18,16},{20... | collective-permute-start | bytes 442376 | tf_op jit(solution)/shard_map/ppermute | solution.py:15
  142.4 3.9 %collective-permute-done.13 = bf16[1,192,384]{2,1,0:T(8,128)(2,1)S(1)} collective-permute-done((bf16[1,192,384]{2,1,0:T(8,128)(2,1)S(1)}, bf16[1,192,384]{2,1,0:T(8,128)(2,1)S(1)}, u32[]{:S(2)}, u32[]{:S(2)}) %collective-permute-start.13) | collective-permute-done | bytes 147488 | tf_op jit(solution)/shard_map/ppermute | solution.py:15
  146.4 0.5 convolution_convert_fusion
  147.1 2.9 %collective-permute-start.16 = (bf16[1,192,384]{2,1,0:T(8,128)(2,1)S(1)}, bf16[1,192,384]{2,1,0:T(8,128)(2,1)S(1)}, u32[]{:S(2)}, u32[]{:S(2)}) collective-permute-start(bf16[1,192,384]{2,1,0:T(8,128)(2,1)S(1)} %get-tuple-element.7), channel_id=1, source_target_pairs={{0,2},{2,4},{4,6},{6,8},{8,10},{10,12},{12,14},{14,16},{16,18},{18... | collective-permute-start | bytes 442376 | tf_op jit(solution)/shard_map/ppermute | solution.py:12
  149.9 1.3 collective-permute-start.19
  151.2 3.0 %collective-permute-start.18 = (bf16[1,192,384]{2,1,0:T(8,128)(2,1)S(1)}, bf16[1,192,384]{2,1,0:T(8,128)(2,1)S(1)}, u32[]{:S(2)}, u32[]{:S(2)}) collective-permute-start(bf16[1,192,384]{2,1,0:T(8,128)(2,1)S(1)} %get-tuple-element.9), channel_id=1, source_target_pairs={{0,1},{2,3},{4,5},{6,7},{8,9},{10,11},{12,13},{14,15},{16,17},{18,... | collective-permute-start | bytes 442376 | tf_op jit(solution)/shard_map/ppermute | solution.py:12
  154.3 3.4 %collective-permute-start.17 = (bf16[1,192,384]{2,1,0:T(8,128)(2,1)S(1)}, bf16[1,192,384]{2,1,0:T(8,128)(2,1)S(1)}, u32[]{:S(2)}, u32[]{:S(2)}) collective-permute-start(bf16[1,192,384]{2,1,0:T(8,128)(2,1)S(1)} %get-tuple-element.10), channel_id=1, source_target_pairs={{2,0},{4,2},{6,4},{8,6},{10,8},{12,10},{14,12},{16,14},{18,16},{20... | collective-permute-start | bytes 442376 | tf_op jit(solution)/shard_map/ppermute | solution.py:15
  157.8 0.6 multiply_reduce_fusion.1
  158.4 3.8 %collective-permute-done.17 = bf16[1,192,384]{2,1,0:T(8,128)(2,1)S(1)} collective-permute-done((bf16[1,192,384]{2,1,0:T(8,128)(2,1)S(1)}, bf16[1,192,384]{2,1,0:T(8,128)(2,1)S(1)}, u32[]{:S(2)}, u32[]{:S(2)}) %collective-permute-start.17) | collective-permute-done | bytes 147488 | tf_op jit(solution)/shard_map/ppermute | solution.py:15
  162.2 0.4 multiply_reduce_fusion
  162.6 45.2 %all-reduce = (f32[192]{0:T(256)S(1)}, f32[192]{0:T(256)S(1)}) all-reduce(f32[192]{0:T(256)S(1)} %multiply_reduce_fusion.1, f32[192]{0:T(256)S(1)} %multiply_reduce_fusion), channel_id=1, replica_groups=mesh['gx'=16,'gy'=2] {'gx','gy'}, use_global_device_ids=true, to_apply=%region_1.0 | all-reduce | flops 384 | bytes 3072 | tf_op jit(solution)/shard_map/psum | solution.py:80
  207.9 2.3 %fusion.30 = bf16[1,1,4,192,384]{4,3,2,1,0:T(8,128)(2,1)} fusion(bf16[4,192,384]{2,1,0:T(8,128)(2,1)S(1)} %convolution_convert_fusion.1, bf16[4,192,384]{2,1,0:T(8,128)(2,1)S(1)} %convolution_convert_fusion.4, f32[192]{0:T(256)S(1)} %div.3, bf16[1,192,384]{2,1,0:T(8,128)(2,1)S(1)} %copy-done.26, bf16[1,192,384]{2,1,0:T(8,128)(2,1)S(1)} %copy-done.28, ...), kind=kLoop, calls=%fused_computation.46 | loop fusion | flops 4423680 | bytes 2949888 | tf_op jit(solution)/shard_map/broadcast_in_dim | solution.py:85
  (110 shorter events, 0.7 us)
Async XLA Ops:
  0.0 12.9 %copy-start = (bf16[1,1,4,384,384]{4,3,2,1,0:T(8,128)(2,1)S(1)}, bf16[1,1,4,384,384]{4,3,2,1,0:T(8,128)(2,1)}, u32[]{:S(2)}) copy-start(bf16[1,1,4,384,384]{4,3,2,1,0:T(8,128)(2,1)} %param.9) | copy-start | bytes 3538948
  0.0 13.0 %copy-start.2 = (bf16[1,1,4,192,384]{4,3,2,1,0:T(8,128)(2,1)S(1)}, bf16[1,1,4,192,384]{4,3,2,1,0:T(8,128)(2,1)}, u32[]{:S(2)}) copy-start(bf16[1,1,4,192,384]{4,3,2,1,0:T(8,128)(2,1)} %param.7) | copy-start | bytes 1769476
  0.0 11.5 %copy-start.43 = (s32[1,1,4]{2,1,0:T(1,128)S(1)}, s32[1,1,4]{2,1,0:T(1,128)}, u32[]{:S(2)}) copy-start(s32[1,1,4]{2,1,0:T(1,128)} %param.13) | copy-start | bytes 52
  1.3 10.8 %collective-permute-start = (bf16[1,192,384]{2,1,0:T(8,128)(2,1)S(1)}, bf16[1,192,384]{2,1,0:T(8,128)(2,1)S(1)}, u32[]{:S(2)}, u32[]{:S(2)}) collective-permute-start(bf16[1,192,384]{2,1,0:T(8,128)(2,1)S(1)} %get-tuple-element.23), channel_id=1, source_target_pairs={{0,2},{2,4},{4,6},{6,8},{8,10},{10,12},{12,14},{14,16},{16,18},{18... | collective-permute-start | bytes 442376 | tf_op jit(solution)/shard_map/ppermute | solution.py:12
  4.7 8.2 %collective-permute-start.1 = (bf16[1,192,384]{2,1,0:T(8,128)(2,1)S(1)}, bf16[1,192,384]{2,1,0:T(8,128)(2,1)S(1)}, u32[]{:S(2)}, u32[]{:S(2)}) collective-permute-start(bf16[1,192,384]{2,1,0:T(8,128)(2,1)S(1)} %get-tuple-element.24), channel_id=1, source_target_pairs={{2,0},{4,2},{6,4},{8,6},{10,8},{12,10},{14,12},{16,14},{18,16},{20... | collective-permute-start | bytes 442376 | tf_op jit(solution)/shard_map/ppermute | solution.py:15
  7.2 5.7 %collective-permute-start.3 = (bf16[1,192,384]{2,1,0:T(8,128)(2,1)S(1)}, bf16[1,192,384]{2,1,0:T(8,128)(2,1)S(1)}, u32[]{:S(2)}, u32[]{:S(2)}) collective-permute-start(bf16[1,192,384]{2,1,0:T(8,128)(2,1)S(1)} %get-tuple-element.25), channel_id=1, source_target_pairs={{1,0},{3,2},{5,4},{7,6},{9,8},{11,10},{13,12},{15,14},{17,16},{19,... | collective-permute-start | bytes 442376 | tf_op jit(solution)/shard_map/ppermute | solution.py:15
  8.5 4.5 %collective-permute-start.2 = (bf16[1,192,384]{2,1,0:T(8,128)(2,1)S(1)}, bf16[1,192,384]{2,1,0:T(8,128)(2,1)S(1)}, u32[]{:S(2)}, u32[]{:S(2)}) collective-permute-start(bf16[1,192,384]{2,1,0:T(8,128)(2,1)S(1)} %get-tuple-element.26), channel_id=1, source_target_pairs={{0,1},{2,3},{4,5},{6,7},{8,9},{10,11},{12,13},{14,15},{16,17},{18,... | collective-permute-start | bytes 442376 | tf_op jit(solution)/shard_map/ppermute | solution.py:12
  13.0 36.6 %copy-start.1 = (bf16[1,1,4,384,384]{4,3,2,1,0:T(8,128)(2,1)S(1)}, bf16[1,1,4,384,384]{4,3,2,1,0:T(8,128)(2,1)}, u32[]{:S(2)}) copy-start(bf16[1,1,4,384,384]{4,3,2,1,0:T(8,128)(2,1)} %param.10) | copy-start | bytes 3538948
  55.9 15.9 %copy-start.41 = (bf16[1,1,4,384,384]{4,3,2,1,0:T(8,128)(2,1)S(1)}, bf16[1,1,4,384,384]{4,3,2,1,0:T(8,128)(2,1)}, u32[]{:S(2)}) copy-start(bf16[1,1,4,384,384]{4,3,2,1,0:T(8,128)(2,1)} %param.8) | copy-start | bytes 3538948
  56.0 12.5 %collective-permute-start.4 = (bf16[1,192,384]{2,1,0:T(8,128)(2,1)S(1)}, bf16[1,192,384]{2,1,0:T(8,128)(2,1)S(1)}, u32[]{:S(2)}, u32[]{:S(2)}) collective-permute-start(bf16[1,192,384]{2,1,0:T(8,128)(2,1)S(1)} %get-tuple-element.19), channel_id=1, source_target_pairs={{0,2},{2,4},{4,6},{6,8},{8,10},{10,12},{12,14},{14,16},{16,18},{18... | collective-permute-start | bytes 442376 | tf_op jit(solution)/shard_map/ppermute | solution.py:12
  59.5 9.0 %collective-permute-start.7 = (bf16[1,192,384]{2,1,0:T(8,128)(2,1)S(1)}, bf16[1,192,384]{2,1,0:T(8,128)(2,1)S(1)}, u32[]{:S(2)}, u32[]{:S(2)}) collective-permute-start(bf16[1,192,384]{2,1,0:T(8,128)(2,1)S(1)} %get-tuple-element.20), channel_id=1, source_target_pairs={{1,0},{3,2},{5,4},{7,6},{9,8},{11,10},{13,12},{15,14},{17,16},{19,... | collective-permute-start | bytes 442376 | tf_op jit(solution)/shard_map/ppermute | solution.py:15
  60.8 7.7 %collective-permute-start.6 = (bf16[1,192,384]{2,1,0:T(8,128)(2,1)S(1)}, bf16[1,192,384]{2,1,0:T(8,128)(2,1)S(1)}, u32[]{:S(2)}, u32[]{:S(2)}) collective-permute-start(bf16[1,192,384]{2,1,0:T(8,128)(2,1)S(1)} %get-tuple-element.21), channel_id=1, source_target_pairs={{0,1},{2,3},{4,5},{6,7},{8,9},{10,11},{12,13},{14,15},{16,17},{18,... | collective-permute-start | bytes 442376 | tf_op jit(solution)/shard_map/ppermute | solution.py:12
  63.9 7.9 %collective-permute-start.5 = (bf16[1,192,384]{2,1,0:T(8,128)(2,1)S(1)}, bf16[1,192,384]{2,1,0:T(8,128)(2,1)S(1)}, u32[]{:S(2)}, u32[]{:S(2)}) collective-permute-start(bf16[1,192,384]{2,1,0:T(8,128)(2,1)S(1)} %get-tuple-element.22), channel_id=1, source_target_pairs={{2,0},{4,2},{6,4},{8,6},{10,8},{12,10},{14,12},{16,14},{18,16},{20... | collective-permute-start | bytes 442376 | tf_op jit(solution)/shard_map/ppermute | solution.py:15
  72.5 17.4 %copy-start.4 = (bf16[4,192,384]{2,1,0:T(8,128)(2,1)}, bf16[4,192,384]{2,1,0:T(8,128)(2,1)S(1)}, u32[]{:S(2)}) copy-start(bf16[4,192,384]{2,1,0:T(8,128)(2,1)S(1)} %convolution_convert_fusion.3) | copy-start | bytes 1769476
  72.5 16.7 %copy-start.12 = (bf16[1,192,384]{2,1,0:T(8,128)(2,1)S(1)}, bf16[1,192,384]{2,1,0:T(8,128)(2,1)}, u32[]{:S(2)}) copy-start(bf16[1,192,384]{2,1,0:T(8,128)(2,1)} %copy-done.11) | copy-start | bytes 442372
  72.5 16.7 %copy-start.15 = (bf16[1,192,384]{2,1,0:T(8,128)(2,1)S(1)}, bf16[1,192,384]{2,1,0:T(8,128)(2,1)}, u32[]{:S(2)}) copy-start(bf16[1,192,384]{2,1,0:T(8,128)(2,1)} %copy-done.14) | copy-start | bytes 442372
  72.5 16.7 %copy-start.18 = (bf16[1,192,384]{2,1,0:T(8,128)(2,1)S(1)}, bf16[1,192,384]{2,1,0:T(8,128)(2,1)}, u32[]{:S(2)}) copy-start(bf16[1,192,384]{2,1,0:T(8,128)(2,1)} %copy-done.17) | copy-start | bytes 442372
  72.5 16.7 %copy-start.21 = (bf16[1,192,384]{2,1,0:T(8,128)(2,1)S(1)}, bf16[1,192,384]{2,1,0:T(8,128)(2,1)}, u32[]{:S(2)}) copy-start(bf16[1,192,384]{2,1,0:T(8,128)(2,1)} %copy-done.20) | copy-start | bytes 442372
  72.6 11.5 %collective-permute-start.8 = (bf16[1,192,384]{2,1,0:T(8,128)(2,1)S(1)}, bf16[1,192,384]{2,1,0:T(8,128)(2,1)S(1)}, u32[]{:S(2)}, u32[]{:S(2)}) collective-permute-start(bf16[1,192,384]{2,1,0:T(8,128)(2,1)S(1)} %get-tuple-element.15), channel_id=1, source_target_pairs={{0,2},{2,4},{4,6},{6,8},{8,10},{10,12},{12,14},{14,16},{16,18},{18... | collective-permute-start | bytes 442376 | tf_op jit(solution)/shard_map/ppermute | solution.py:12
  76.1 8.0 %collective-permute-start.11 = (bf16[1,192,384]{2,1,0:T(8,128)(2,1)S(1)}, bf16[1,192,384]{2,1,0:T(8,128)(2,1)S(1)}, u32[]{:S(2)}, u32[]{:S(2)}) collective-permute-start(bf16[1,192,384]{2,1,0:T(8,128)(2,1)S(1)} %get-tuple-element.16), channel_id=1, source_target_pairs={{1,0},{3,2},{5,4},{7,6},{9,8},{11,10},{13,12},{15,14},{17,16},{19,... | collective-permute-start | bytes 442376 | tf_op jit(solution)/shard_map/ppermute | solution.py:15
  77.4 6.7 %collective-permute-start.10 = (bf16[1,192,384]{2,1,0:T(8,128)(2,1)S(1)}, bf16[1,192,384]{2,1,0:T(8,128)(2,1)S(1)}, u32[]{:S(2)}, u32[]{:S(2)}) collective-permute-start(bf16[1,192,384]{2,1,0:T(8,128)(2,1)S(1)} %get-tuple-element.17), channel_id=1, source_target_pairs={{0,1},{2,3},{4,5},{6,7},{8,9},{10,11},{12,13},{14,15},{16,17},{18,... | collective-permute-start | bytes 442376 | tf_op jit(solution)/shard_map/ppermute | solution.py:12
  80.4 8.7 %collective-permute-start.9 = (bf16[1,192,384]{2,1,0:T(8,128)(2,1)S(1)}, bf16[1,192,384]{2,1,0:T(8,128)(2,1)S(1)}, u32[]{:S(2)}, u32[]{:S(2)}) collective-permute-start(bf16[1,192,384]{2,1,0:T(8,128)(2,1)S(1)} %get-tuple-element.18), channel_id=1, source_target_pairs={{2,0},{4,2},{6,4},{8,6},{10,8},{12,10},{14,12},{16,14},{18,16},{20... | collective-permute-start | bytes 442376 | tf_op jit(solution)/shard_map/ppermute | solution.py:15
  131.9 14.4 %copy-start.42 = (bf16[1,1,4,384,384]{4,3,2,1,0:T(8,128)(2,1)S(1)}, bf16[1,1,4,384,384]{4,3,2,1,0:T(8,128)(2,1)}, u32[]{:S(2)}) copy-start(bf16[1,1,4,384,384]{4,3,2,1,0:T(8,128)(2,1)} %param.8) | copy-start | bytes 3538948
  132.0 10.3 %collective-permute-start.12 = (bf16[1,192,384]{2,1,0:T(8,128)(2,1)S(1)}, bf16[1,192,384]{2,1,0:T(8,128)(2,1)S(1)}, u32[]{:S(2)}, u32[]{:S(2)}) collective-permute-start(bf16[1,192,384]{2,1,0:T(8,128)(2,1)S(1)} %get-tuple-element.11), channel_id=1, source_target_pairs={{0,2},{2,4},{4,6},{6,8},{8,10},{10,12},{12,14},{14,16},{16,18},{18... | collective-permute-start | bytes 442376 | tf_op jit(solution)/shard_map/ppermute | solution.py:12
  134.1 8.3 %collective-permute-start.15 = (bf16[1,192,384]{2,1,0:T(8,128)(2,1)S(1)}, bf16[1,192,384]{2,1,0:T(8,128)(2,1)S(1)}, u32[]{:S(2)}, u32[]{:S(2)}) collective-permute-start(bf16[1,192,384]{2,1,0:T(8,128)(2,1)S(1)} %get-tuple-element.12), channel_id=1, source_target_pairs={{1,0},{3,2},{5,4},{7,6},{9,8},{11,10},{13,12},{15,14},{17,16},{19,... | collective-permute-start | bytes 442376 | tf_op jit(solution)/shard_map/ppermute | solution.py:15
  135.4 7.0 %collective-permute-start.14 = (bf16[1,192,384]{2,1,0:T(8,128)(2,1)S(1)}, bf16[1,192,384]{2,1,0:T(8,128)(2,1)S(1)}, u32[]{:S(2)}, u32[]{:S(2)}) collective-permute-start(bf16[1,192,384]{2,1,0:T(8,128)(2,1)S(1)} %get-tuple-element.13), channel_id=1, source_target_pairs={{0,1},{2,3},{4,5},{6,7},{8,9},{10,11},{12,13},{14,15},{16,17},{18,... | collective-permute-start | bytes 442376 | tf_op jit(solution)/shard_map/ppermute | solution.py:12
  138.4 7.9 %collective-permute-start.13 = (bf16[1,192,384]{2,1,0:T(8,128)(2,1)S(1)}, bf16[1,192,384]{2,1,0:T(8,128)(2,1)S(1)}, u32[]{:S(2)}, u32[]{:S(2)}) collective-permute-start(bf16[1,192,384]{2,1,0:T(8,128)(2,1)S(1)} %get-tuple-element.14), channel_id=1, source_target_pairs={{2,0},{4,2},{6,4},{8,6},{10,8},{12,10},{14,12},{16,14},{18,16},{20... | collective-permute-start | bytes 442376 | tf_op jit(solution)/shard_map/ppermute | solution.py:15
  142.4 19.9 %copy-start.6 = (bf16[1,192,384]{2,1,0:T(8,128)(2,1)}, bf16[1,192,384]{2,1,0:T(8,128)(2,1)S(1)}, u32[]{:S(2)}) copy-start(bf16[1,192,384]{2,1,0:T(8,128)(2,1)S(1)} %collective-permute-done.12) | copy-start | bytes 442372
  142.4 19.8 %copy-start.7 = (bf16[1,192,384]{2,1,0:T(8,128)(2,1)}, bf16[1,192,384]{2,1,0:T(8,128)(2,1)S(1)}, u32[]{:S(2)}) copy-start(bf16[1,192,384]{2,1,0:T(8,128)(2,1)S(1)} %collective-permute-done.15) | copy-start | bytes 442372
  142.4 19.8 %copy-start.8 = (bf16[1,192,384]{2,1,0:T(8,128)(2,1)}, bf16[1,192,384]{2,1,0:T(8,128)(2,1)S(1)}, u32[]{:S(2)}) copy-start(bf16[1,192,384]{2,1,0:T(8,128)(2,1)S(1)} %collective-permute-done.14) | copy-start | bytes 442372
  146.4 15.9 %copy-start.9 = (bf16[1,192,384]{2,1,0:T(8,128)(2,1)}, bf16[1,192,384]{2,1,0:T(8,128)(2,1)S(1)}, u32[]{:S(2)}) copy-start(bf16[1,192,384]{2,1,0:T(8,128)(2,1)S(1)} %collective-permute-done.13) | copy-start | bytes 442372
  146.4 11.3 %copy-start.13 = (bf16[1,192,384]{2,1,0:T(8,128)(2,1)S(1)}, bf16[1,192,384]{2,1,0:T(8,128)(2,1)}, u32[]{:S(2)}) copy-start(bf16[1,192,384]{2,1,0:T(8,128)(2,1)} %copy-done.11) | copy-start | bytes 442372
  146.4 11.3 %copy-start.16 = (bf16[1,192,384]{2,1,0:T(8,128)(2,1)S(1)}, bf16[1,192,384]{2,1,0:T(8,128)(2,1)}, u32[]{:S(2)}) copy-start(bf16[1,192,384]{2,1,0:T(8,128)(2,1)} %copy-done.14) | copy-start | bytes 442372
  146.4 11.3 %copy-start.19 = (bf16[1,192,384]{2,1,0:T(8,128)(2,1)S(1)}, bf16[1,192,384]{2,1,0:T(8,128)(2,1)}, u32[]{:S(2)}) copy-start(bf16[1,192,384]{2,1,0:T(8,128)(2,1)} %copy-done.17) | copy-start | bytes 442372
  146.4 11.3 %copy-start.22 = (bf16[1,192,384]{2,1,0:T(8,128)(2,1)S(1)}, bf16[1,192,384]{2,1,0:T(8,128)(2,1)}, u32[]{:S(2)}) copy-start(bf16[1,192,384]{2,1,0:T(8,128)(2,1)} %copy-done.20) | copy-start | bytes 442372
  146.4 11.3 %copy-start.32 = (bf16[1,192,384]{2,1,0:T(8,128)(2,1)S(1)}, bf16[1,192,384]{2,1,0:T(8,128)(2,1)}, u32[]{:S(2)}) copy-start(bf16[1,192,384]{2,1,0:T(8,128)(2,1)} %copy-done.31) | copy-start | bytes 442372
  146.4 11.3 %copy-start.34 = (bf16[1,192,384]{2,1,0:T(8,128)(2,1)S(1)}, bf16[1,192,384]{2,1,0:T(8,128)(2,1)}, u32[]{:S(2)}) copy-start(bf16[1,192,384]{2,1,0:T(8,128)(2,1)} %copy-done.33) | copy-start | bytes 442372
  146.4 11.3 %copy-start.36 = (bf16[1,192,384]{2,1,0:T(8,128)(2,1)S(1)}, bf16[1,192,384]{2,1,0:T(8,128)(2,1)}, u32[]{:S(2)}) copy-start(bf16[1,192,384]{2,1,0:T(8,128)(2,1)} %copy-done.35) | copy-start | bytes 442372
  146.4 11.3 %copy-start.38 = (bf16[1,192,384]{2,1,0:T(8,128)(2,1)S(1)}, bf16[1,192,384]{2,1,0:T(8,128)(2,1)}, u32[]{:S(2)}) copy-start(bf16[1,192,384]{2,1,0:T(8,128)(2,1)} %copy-done.37) | copy-start | bytes 442372
  147.0 10.8 %copy-start.3 = (bf16[1,1,4,192,384]{4,3,2,1,0:T(8,128)(2,1)S(1)}, bf16[1,1,4,192,384]{4,3,2,1,0:T(8,128)(2,1)}, u32[]{:S(2)}) copy-start(bf16[1,1,4,192,384]{4,3,2,1,0:T(8,128)(2,1)} %param.7) | copy-start | bytes 1769476
  147.1 11.3 %collective-permute-start.16 = (bf16[1,192,384]{2,1,0:T(8,128)(2,1)S(1)}, bf16[1,192,384]{2,1,0:T(8,128)(2,1)S(1)}, u32[]{:S(2)}, u32[]{:S(2)}) collective-permute-start(bf16[1,192,384]{2,1,0:T(8,128)(2,1)S(1)} %get-tuple-element.7), channel_id=1, source_target_pairs={{0,2},{2,4},{4,6},{6,8},{8,10},{10,12},{12,14},{14,16},{16,18},{18... | collective-permute-start | bytes 442376 | tf_op jit(solution)/shard_map/ppermute | solution.py:12
  149.9 8.4 %collective-permute-start.19 = (bf16[1,192,384]{2,1,0:T(8,128)(2,1)S(1)}, bf16[1,192,384]{2,1,0:T(8,128)(2,1)S(1)}, u32[]{:S(2)}, u32[]{:S(2)}) collective-permute-start(bf16[1,192,384]{2,1,0:T(8,128)(2,1)S(1)} %get-tuple-element.8), channel_id=1, source_target_pairs={{1,0},{3,2},{5,4},{7,6},{9,8},{11,10},{13,12},{15,14},{17,16},{19,... | collective-permute-start | bytes 442376 | tf_op jit(solution)/shard_map/ppermute | solution.py:15
  151.2 7.1 %collective-permute-start.18 = (bf16[1,192,384]{2,1,0:T(8,128)(2,1)S(1)}, bf16[1,192,384]{2,1,0:T(8,128)(2,1)S(1)}, u32[]{:S(2)}, u32[]{:S(2)}) collective-permute-start(bf16[1,192,384]{2,1,0:T(8,128)(2,1)S(1)} %get-tuple-element.9), channel_id=1, source_target_pairs={{0,1},{2,3},{4,5},{6,7},{8,9},{10,11},{12,13},{14,15},{16,17},{18,... | collective-permute-start | bytes 442376 | tf_op jit(solution)/shard_map/ppermute | solution.py:12
  154.3 7.9 %collective-permute-start.17 = (bf16[1,192,384]{2,1,0:T(8,128)(2,1)S(1)}, bf16[1,192,384]{2,1,0:T(8,128)(2,1)S(1)}, u32[]{:S(2)}, u32[]{:S(2)}) collective-permute-start(bf16[1,192,384]{2,1,0:T(8,128)(2,1)S(1)} %get-tuple-element.10), channel_id=1, source_target_pairs={{2,0},{4,2},{6,4},{8,6},{10,8},{12,10},{14,12},{16,14},{18,16},{20... | collective-permute-start | bytes 442376 | tf_op jit(solution)/shard_map/ppermute | solution.py:15
  158.3 49.5 %copy-start.24 = (bf16[1,192,384]{2,1,0:T(8,128)(2,1)S(1)}, bf16[1,192,384]{2,1,0:T(8,128)(2,1)}, u32[]{:S(2)}) copy-start(bf16[1,192,384]{2,1,0:T(8,128)(2,1)} %copy-done.23) | copy-start | bytes 442372
  158.3 49.5 %copy-start.26 = (bf16[1,192,384]{2,1,0:T(8,128)(2,1)S(1)}, bf16[1,192,384]{2,1,0:T(8,128)(2,1)}, u32[]{:S(2)}) copy-start(bf16[1,192,384]{2,1,0:T(8,128)(2,1)} %copy-done.25) | copy-start | bytes 442372
  158.3 49.5 %copy-start.28 = (bf16[1,192,384]{2,1,0:T(8,128)(2,1)S(1)}, bf16[1,192,384]{2,1,0:T(8,128)(2,1)}, u32[]{:S(2)}) copy-start(bf16[1,192,384]{2,1,0:T(8,128)(2,1)} %copy-done.27) | copy-start | bytes 442372
  158.4 49.5 %copy-start.30 = (bf16[1,192,384]{2,1,0:T(8,128)(2,1)S(1)}, bf16[1,192,384]{2,1,0:T(8,128)(2,1)}, u32[]{:S(2)}) copy-start(bf16[1,192,384]{2,1,0:T(8,128)(2,1)} %copy-done.29) | copy-start | bytes 442372
  (16 other events, 49.2 us)
where the time goes:
time: 211 us; the launch traced here: 210 us
  blocking collectives  115 us (55%)
  starting transfers between devices  55 us (26%)
  waiting for transfers between devices  16.9 us (8%)
  matrix products  15.6 us (7%)
  other arithmetic  3.87 us (2%)
  local copies, waits for them, and re-layouts  3.46 us (2%)
    all_gather x2, blocking collectives, precondition(): lax.all_gather(primal, ('gx', 'gy'), axis=0, tiled=True)  69.4 us
    psum x1, blocking collectives, per_device(): top = lax.psum(jnp.sum(resid1 * second, axis=(0, 2)), ('gx', 'gy'))  45.2 us
    ppermute x10, starting transfers between devices, with_halo(): lax.ppermute(lax.slice_in_dim(block, block.shape[dim] - width, None, axis...  30.5 us
    ppermute x10, starting transfers between devices, with_halo(): lax.ppermute(lax.slice_in_dim(block, 0, width, axis=dim), axis, backward)  24.4 us
    ppermute x10, waiting for transfers between devices, with_halo(): lax.ppermute(lax.slice_in_dim(block, 0, width, axis=dim), axis, backward)  16.8 us
    dot_general x6, matrix products, face_mul(): jnp.einsum('fry,fyx->frx', vectors, matrices, preferred_element_type=jnp....  9.97 us
  transfers between devices with their start and end apart: 20, of which 5 were waited for; matrix products, arithmetic and copies ran while one was open for 1% of the time, Pallas kernels for 0%

commit v1 on v0

--- a/solution.py
+++ b/solution.py
@@ -2,6 +2,18 @@
 import jax.numpy as jnp
 from jax import lax
 from jax.sharding import PartitionSpec as P
+
+
+def gather_by_bits(x, axis, dim):
+    ways, here, turn = (lax.axis_size(axis), lax.axis_index(axis), x.shape[dim])
+    line, have = (x, 1)
+    while have < ways:
+        line = jnp.concatenate(
+            [line, lax.ppermute(line, axis, [(d, (d - have) % ways) for d in range(ways)])],
+            axis=dim,
+        )
+        have = 2 * have
+    return jnp.roll(line, here * turn, axis=dim)
 
 
 def with_halo(block, sides, width):
@@ -63,7 +75,7 @@
         primal = jnp.einsum(
             "kfx,frx->kr", picks_half, scaled, preferred_element_type=jnp.float32
         ).astype(jnp.bfloat16)
-        coarse = add_coarse(lax.all_gather(primal, ("gx", "gy"), axis=0, tiled=True))
+        coarse = add_coarse(gather_by_bits(primal, ("gx", "gy"), 0))
         placed = jnp.einsum("kfx,kr->frx", picks_full, coarse, precision=lax.Precision.HIGHEST)
         weighted = (softened + placed).astype(jnp.bfloat16)
         spread = face_mul(weighted, deluxe_panel).astype(jnp.bfloat16)

time: 211 us -> 194 us (0.919); the launches traced: 210 us -> 191 us
  blocking collectives: 115 us -> 39.6 us
  waiting for transfers between devices: 16.9 us -> 44 us
  starting transfers between devices: 55 us -> 72.9 us
  local copies, waits for them, and re-layouts: 3.46 us -> 10.4 us
  matrix products: 15.6 us -> 18.3 us
    all_gather x2 -> x0, blocking collectives: 69.4 us -> none  [precondition(): lax.all_gather(primal, ('gx', 'gy'), axis=0, tiled=True)]
    ppermute x0 -> x10, starting transfers between devices: none -> 20.9 us  [gather_by_bits(): lax.ppermute(line, axis, [(d, (d - have) % ways) for d in range(ways)])]
    ppermute x0 -> x10, waiting for transfers between devices: none -> 18.4 us  [gather_by_bits(): lax.ppermute(line, axis, [(d, (d - have) % ways) for d in range(ways)])]
    ppermute x10, waiting for transfers between devices: 16.8 us -> 25.6 us  [with_halo(): lax.ppermute(lax.slice_in_dim(block, 0, width, axis=dim), axis, backward)]
    concatenate x0 -> x4, local copies, waits for them, and re-layouts: none -> 7.42 us  [gather_by_bits(): jnp.concatenate([line, lax.ppermute(line, axis, [(d, (d - have) % ways) f...]
    ppermute x10, starting transfers between devices: 24.4 us -> 17.9 us  [with_halo(): lax.ppermute(lax.slice_in_dim(block, 0, width, axis=dim), axis, backward)]
    psum x1, blocking collectives: 45.2 us -> 39.6 us  [per_device(): top = lax.psum(jnp.sum(resid1 * second, axis=(0, 2)), ('gx', 'gy'))]
    ppermute x10, starting transfers between devices: 30.5 us -> 34 us  [with_halo(): lax.ppermute(lax.slice_in_dim(block, block.shape[dim] - width, None, axis...]
  transfers between devices with their start and end apart: 20 -> 30, of which waited for: 5 -> 14; matrix products, arithmetic and copies ran while one was open for 1% -> 3% of each run, Pallas kernels for 0% -> 0%
where the time goes in v1:
time: 194 us; the launch traced here: 191 us
  starting transfers between devices  72.9 us (38%)
  waiting for transfers between devices  44 us (23%)
  blocking collectives  39.6 us (20%)
  matrix products  18.3 us (9%)
  local copies, waits for them, and re-layouts  10.4 us (5%)
  other arithmetic  4.52 us (2%)
    psum x1, blocking collectives, per_device(): top = lax.psum(jnp.sum(resid1 * second, axis=(0, 2)), ('gx', 'gy'))  39.6 us
    ppermute x10, starting transfers between devices, with_halo(): lax.ppermute(lax.slice_in_dim(block, block.shape[dim] - width, None, axis...  34 us
    ppermute x10, waiting for transfers between devices, with_halo(): lax.ppermute(lax.slice_in_dim(block, 0, width, axis=dim), axis, backward)  25.6 us
    ppermute x10, starting transfers between devices, gather_by_bits(): lax.ppermute(line, axis, [(d, (d - have) % ways) for d in range(ways)])  20.9 us
    ppermute x10, waiting for transfers between devices, gather_by_bits(): lax.ppermute(line, axis, [(d, (d - have) % ways) for d in range(ways)])  18.4 us
    ppermute x10, starting transfers between devices, with_halo(): lax.ppermute(lax.slice_in_dim(block, 0, width, axis=dim), axis, backward)  17.9 us
    dot_general x6, matrix products, face_mul(): jnp.einsum('fry,fyx->frx', vectors, matrices, preferred_element_type=jnp....  11 us
    concatenate x4, local copies, waits for them, and re-layouts, gather_by_bits(): jnp.concatenate([line, lax.ppermute(line, axis, [(d, (d - have) % ways) f...  7.42 us
  transfers between devices with their start and end apart: 30, of which 14 were waited for; matrix products, arithmetic and copies ran while one was open for 3% of the time, Pallas kernels for 0%

profile of v1, /device:TPU:10, one launch (start us, length us, event | category | flops | bytes accessed | tf_op | source)
XLA Modules:
  0.0 190.5 jit_solution(9056369682015020239)
XLA Ops:
  0.0 1.3 slice_bitcast_fusion.3
  1.3 3.4 %collective-permute-start = (bf16[1,192,384]{2,1,0:T(8,128)(2,1)S(1)}, bf16[1,192,384]{2,1,0:T(8,128)(2,1)S(1)}, u32[]{:S(2)}, u32[]{:S(2)}) collective-permute-start(bf16[1,192,384]{2,1,0:T(8,128)(2,1)S(1)} %get-tuple-element.24), channel_id=1, source_target_pairs={{0,2},{2,4},{4,6},{6,8},{8,10},{10,12},{12,14},{14,16},{16,18},{18... | collective-permute-start | bytes 442376 | tf_op jit(solution)/shard_map/ppermute | solution.py:24
  4.7 2.4 %collective-permute-start.1 = (bf16[1,192,384]{2,1,0:T(8,128)(2,1)S(1)}, bf16[1,192,384]{2,1,0:T(8,128)(2,1)S(1)}, u32[]{:S(2)}, u32[]{:S(2)}) collective-permute-start(bf16[1,192,384]{2,1,0:T(8,128)(2,1)S(1)} %get-tuple-element.25), channel_id=1, source_target_pairs={{2,0},{4,2},{6,4},{8,6},{10,8},{12,10},{14,12},{16,14},{18,16},{20... | collective-permute-start | bytes 442376 | tf_op jit(solution)/shard_map/ppermute | solution.py:27
  8.5 3.0 %collective-permute-start.2 = (bf16[1,192,384]{2,1,0:T(8,128)(2,1)S(1)}, bf16[1,192,384]{2,1,0:T(8,128)(2,1)S(1)}, u32[]{:S(2)}, u32[]{:S(2)}) collective-permute-start(bf16[1,192,384]{2,1,0:T(8,128)(2,1)S(1)} %get-tuple-element.27), channel_id=1, source_target_pairs={{0,1},{2,3},{4,5},{6,7},{8,9},{10,11},{12,13},{14,15},{16,17},{18,... | collective-permute-start | bytes 442376 | tf_op jit(solution)/shard_map/ppermute | solution.py:24
  11.6 1.3 collective-permute-done.1
  14.0 1.8 collective-permute-start.4
  15.8 1.3 collective-permute-done.4
  17.7 4.0 %collective-permute-done.5 = bf16[8,192]{1,0:T(8,128)(2,1)S(1)} collective-permute-done((bf16[8,192]{1,0:T(8,128)(2,1)S(1)}, bf16[8,192]{1,0:T(8,128)(2,1)S(1)}, u32[]{:S(2)}, u32[]{:S(2)}) %collective-permute-start.5) | collective-permute-done | bytes 3104 | tf_op jit(solution)/shard_map/ppermute | solution.py:12
  21.7 1.5 collective-permute-start.6
  23.1 2.2 %collective-permute-done.6 = bf16[16,192]{1,0:T(8,128)(2,1)S(1)} collective-permute-done((bf16[16,192]{1,0:T(8,128)(2,1)S(1)}, bf16[16,192]{1,0:T(8,128)(2,1)S(1)}, u32[]{:S(2)}, u32[]{:S(2)}) %collective-permute-start.6) | collective-permute-done | bytes 6176 | tf_op jit(solution)/shard_map/ppermute | solution.py:12
  26.6 4.5 %collective-permute-start.7 = (bf16[32,192]{1,0:T(8,128)(2,1)}, bf16[32,192]{1,0:T(8,128)(2,1)}, u32[]{:S(2)}, u32[]{:S(2)}) collective-permute-start(bf16[32,192]{1,0:T(8,128)(2,1)} %pad_maximum_fusion.5), channel_id=1, source_target_pairs={{0,24},{1,25},{2,26},{3,27},{4,28},{5,29},{6,30},{7,31},{8,0},{9,1... | collective-permute-start | bytes 36872 | tf_op jit(solution)/shard_map/ppermute | solution.py:12
  32.8 4.5 %concatenate.44 = bf16[64,192]{1,0:T(8,128)(2,1)} concatenate(bf16[4,192]{1,0:T(4,128)(2,1)S(1)} %fusion.22, bf16[4,192]{1,0:T(4,128)(2,1)} %copy-done.32, bf16[8,192]{1,0:T(8,128)(2,1)S(1)} %collective-permute-done.5, bf16[16,192]{1,0:T(8,128)(2,1)} %copy-done.31, bf16[32,192]{1,0:T(8,128)(2,1)} %collective-permute-done.7), dimensions={0} | concatenate | bytes 49152 | tf_op jit(solution)/shard_map/concatenate | solution.py:11
  37.3 3.6 %collective-permute-start.8 = (bf16[64,192]{1,0:T(8,128)(2,1)}, bf16[64,192]{1,0:T(8,128)(2,1)}, u32[]{:S(2)}, u32[]{:S(2)}) collective-permute-start(bf16[64,192]{1,0:T(8,128)(2,1)} %concatenate.44), channel_id=1, source_target_pairs={{0,16},{1,17},{2,18},{3,19},{4,20},{5,21},{6,22},{7,23},{8,24},{9,... | collective-permute-start | bytes 73736 | tf_op jit(solution)/shard_map/ppermute | solution.py:12
  40.8 1.6 fusion.14
  43.1 2.9 %concatenate.45 = bf16[128,192]{1,0:T(8,128)(2,1)S(1)} concatenate(bf16[4,192]{1,0:T(4,128)(2,1)S(1)} %fusion.22, bf16[4,192]{1,0:T(4,128)(2,1)} %copy-done.32, bf16[8,192]{1,0:T(8,128)(2,1)S(1)} %collective-permute-done.5, bf16[16,192]{1,0:T(8,128)(2,1)} %copy-done.31, bf16[32,192]{1,0:T(8,128)(2,1)} %collective-permute-done.7, bf16[64,192]{1,0:T(8,128)(2,1)} %collective-permute-done.8), dimensions={0} | concatenate | bytes 98304 | tf_op jit(solution)/shard_map/concatenate | solution.py:11
  47.0 2.3 %convolution_bitcast_fusion.1 = f32[4,192,384]{2,1,0:T(8,128)} fusion(f32[192,4,1]{1,0,2:T(8,128)S(1)} %convolution_bitcast_fusion.3, s32[4,384]{1,0:T(4,128)S(1)} %multiply_add_fusion, s32[4]{0:T(128)} %bitcast.74), kind=kOutput, calls=%fused_computation.7 | convolution fusion | flops 14161920 | bytes 1188880 | tf_op jit(solution)/shard_map/kfx,kr->frx/dot_general | solution.py:79
  49.3 2.9 %convolution_convert_fusion.4 = bf16[4,192,384]{2,1,0:T(8,128)(2,1)S(1)} fusion(f32[4,192,384]{2,1,0:T(8,128)} %convolution_bitcast_fusion.1, f32[4,192,384]{2,1,0:T(8,128)} %fusion.14, bf16[1,1,4,384,384]{4,3,2,1,0:T(8,128)(2,1)S(1)} %copy-done.1, bf16[1,1,4,384,384]{4,3,2,1,0:T(8,128)(2,1)S(1)} %copy-done, f32[4]{0:T(128)} %multiply_bitcast_fusion), kind=kOutput, calls=%fused_computation.14 | convolution fusion | flops 454754304 | bytes 5308432 | tf_op jit(solution)/shard_map/fry,fyx->frx/dot_general | solution.py:33
  52.3 3.4 %collective-permute-start.9 = (bf16[1,192,384]{2,1,0:T(8,128)(2,1)S(1)}, bf16[1,192,384]{2,1,0:T(8,128)(2,1)S(1)}, u32[]{:S(2)}, u32[]{:S(2)}) collective-permute-start(bf16[1,192,384]{2,1,0:T(8,128)(2,1)S(1)} %get-tuple-element.20), channel_id=1, source_target_pairs={{0,2},{2,4},{4,6},{6,8},{8,10},{10,12},{12,14},{14,16},{16,18},{18... | collective-permute-start | bytes 442376 | tf_op jit(solution)/shard_map/ppermute | solution.py:24
  57.0 3.0 %collective-permute-start.11 = (bf16[1,192,384]{2,1,0:T(8,128)(2,1)S(1)}, bf16[1,192,384]{2,1,0:T(8,128)(2,1)S(1)}, u32[]{:S(2)}, u32[]{:S(2)}) collective-permute-start(bf16[1,192,384]{2,1,0:T(8,128)(2,1)S(1)} %get-tuple-element.22), channel_id=1, source_target_pairs={{0,1},{2,3},{4,5},{6,7},{8,9},{10,11},{12,13},{14,15},{16,17},{18,... | collective-permute-start | bytes 442376 | tf_op jit(solution)/shard_map/ppermute | solution.py:24
  60.0 2.6 %collective-permute-start.10 = (bf16[1,192,384]{2,1,0:T(8,128)(2,1)S(1)}, bf16[1,192,384]{2,1,0:T(8,128)(2,1)S(1)}, u32[]{:S(2)}, u32[]{:S(2)}) collective-permute-start(bf16[1,192,384]{2,1,0:T(8,128)(2,1)S(1)} %get-tuple-element.23), channel_id=1, source_target_pairs={{2,0},{4,2},{6,4},{8,6},{10,8},{12,10},{14,12},{16,14},{18,16},{20... | collective-permute-start | bytes 442376 | tf_op jit(solution)/shard_map/ppermute | solution.py:27
  62.7 7.7 %collective-permute-done.10 = bf16[1,192,384]{2,1,0:T(8,128)(2,1)S(1)} collective-permute-done((bf16[1,192,384]{2,1,0:T(8,128)(2,1)S(1)}, bf16[1,192,384]{2,1,0:T(8,128)(2,1)S(1)}, u32[]{:S(2)}, u32[]{:S(2)}) %collective-permute-start.10) | collective-permute-done | bytes 147488 | tf_op jit(solution)/shard_map/ppermute | solution.py:27
  71.2 3.8 %collective-permute-start.13 = (bf16[1,192,384]{2,1,0:T(8,128)(2,1)S(1)}, bf16[1,192,384]{2,1,0:T(8,128)(2,1)S(1)}, u32[]{:S(2)}, u32[]{:S(2)}) collective-permute-start(bf16[1,192,384]{2,1,0:T(8,128)(2,1)S(1)} %get-tuple-element.16), channel_id=1, source_target_pairs={{0,2},{2,4},{4,6},{6,8},{8,10},{10,12},{12,14},{14,16},{16,18},{18... | collective-permute-start | bytes 442376 | tf_op jit(solution)/shard_map/ppermute | solution.py:24
  75.0 1.3 collective-permute-start.16
  76.3 3.0 %collective-permute-start.15 = (bf16[1,192,384]{2,1,0:T(8,128)(2,1)S(1)}, bf16[1,192,384]{2,1,0:T(8,128)(2,1)S(1)}, u32[]{:S(2)}, u32[]{:S(2)}) collective-permute-start(bf16[1,192,384]{2,1,0:T(8,128)(2,1)S(1)} %get-tuple-element.18), channel_id=1, source_target_pairs={{0,1},{2,3},{4,5},{6,7},{8,9},{10,11},{12,13},{14,15},{16,17},{18,... | collective-permute-start | bytes 442376 | tf_op jit(solution)/shard_map/ppermute | solution.py:24
  79.3 2.2 %collective-permute-start.14 = (bf16[1,192,384]{2,1,0:T(8,128)(2,1)S(1)}, bf16[1,192,384]{2,1,0:T(8,128)(2,1)S(1)}, u32[]{:S(2)}, u32[]{:S(2)}) collective-permute-start(bf16[1,192,384]{2,1,0:T(8,128)(2,1)S(1)} %get-tuple-element.19), channel_id=1, source_target_pairs={{2,0},{4,2},{6,4},{8,6},{10,8},{12,10},{14,12},{16,14},{18,16},{20... | collective-permute-start | bytes 442376 | tf_op jit(solution)/shard_map/ppermute | solution.py:27
  81.6 5.7 %collective-permute-done.14 = bf16[1,192,384]{2,1,0:T(8,128)(2,1)S(1)} collective-permute-done((bf16[1,192,384]{2,1,0:T(8,128)(2,1)S(1)}, bf16[1,192,384]{2,1,0:T(8,128)(2,1)S(1)}, u32[]{:S(2)}, u32[]{:S(2)}) %collective-permute-start.14) | collective-permute-done | bytes 147488 | tf_op jit(solution)/shard_map/ppermute | solution.py:27
  88.8 1.3 collective-permute-done.17
  90.4 4.4 %collective-permute-done.18 = bf16[8,192]{1,0:T(8,128)(2,1)S(1)} collective-permute-done((bf16[8,192]{1,0:T(8,128)(2,1)S(1)}, bf16[8,192]{1,0:T(8,128)(2,1)S(1)}, u32[]{:S(2)}, u32[]{:S(2)}) %collective-permute-start.18) | collective-permute-done | bytes 3104 | tf_op jit(solution)/shard_map/ppermute | solution.py:12
  94.8 1.8 collective-permute-start.19
  96.5 2.0 %collective-permute-done.19 = bf16[16,192]{1,0:T(8,128)(2,1)S(1)} collective-permute-done((bf16[16,192]{1,0:T(8,128)(2,1)S(1)}, bf16[16,192]{1,0:T(8,128)(2,1)S(1)}, u32[]{:S(2)}, u32[]{:S(2)}) %collective-permute-start.19) | collective-permute-done | bytes 6176 | tf_op jit(solution)/shard_map/ppermute | solution.py:12
  98.6 2.4 %collective-permute-start.20 = (bf16[32,192]{1,0:T(8,128)(2,1)S(1)}, bf16[32,192]{1,0:T(8,128)(2,1)S(1)}, u32[]{:S(2)}, u32[]{:S(2)}) collective-permute-start(bf16[32,192]{1,0:T(8,128)(2,1)S(1)} %pad_maximum_fusion.6), channel_id=1, source_target_pairs={{0,24},{1,25},{2,26},{3,27},{4,28},{5,29},{6,30},{7,31},{8,0},{9,1... | collective-permute-start | bytes 36872 | tf_op jit(solution)/shard_map/ppermute | solution.py:12
  100.9 1.4 collective-permute-done.20
  102.4 4.6 %collective-permute-start.21 = (bf16[64,192]{1,0:T(8,128)(2,1)S(1)}, bf16[64,192]{1,0:T(8,128)(2,1)S(1)}, u32[]{:S(2)}, u32[]{:S(2)}) collective-permute-start(bf16[64,192]{1,0:T(8,128)(2,1)S(1)} %concatenate.49), channel_id=1, source_target_pairs={{0,16},{1,17},{2,18},{3,19},{4,20},{5,21},{6,22},{7,23},{8,24},{9,... | collective-permute-start | bytes 73736 | tf_op jit(solution)/shard_map/ppermute | solution.py:12
  107.0 2.6 %fusion.10 = f32[4,192,384]{2,1,0:T(8,128)} fusion(bf16[4,192,384]{2,1,0:T(8,128)(2,1)} %copy-done.6, bf16[1,1,4,384,384]{4,3,2,1,0:T(8,128)(2,1)S(1)} %copy-done.1), kind=kOutput, calls=%fused_computation.20 | convolution fusion | flops 226492416 | bytes 2949120 | tf_op jit(solution)/shard_map/fry,fyx->frx/dot_general | solution.py:33
  110.0 1.7 convolution_bitcast_fusion
  111.7 2.9 %convolution_convert_fusion.1 = bf16[4,192,384]{2,1,0:T(8,128)(2,1)S(1)} fusion(f32[4,192,384]{2,1,0:T(8,128)} %convolution_bitcast_fusion, f32[4,192,384]{2,1,0:T(8,128)} %fusion.10, bf16[1,1,4,384,384]{4,3,2,1,0:T(8,128)(2,1)S(1)} %copy-done.1, bf16[1,1,4,384,384]{4,3,2,1,0:T(8,128)(2,1)S(1)} %copy-done, f32[4]{0:T(128)S(1)} %copy-done.36), kind=kOutput, calls=%fused_computation.11 | convolution fusion | flops 454754304 | bytes 5308432 | tf_op jit(solution)/shard_map/fry,fyx->frx/dot_general | solution.py:33
  114.7 4.6 %collective-permute-start.22 = (bf16[1,192,384]{2,1,0:T(8,128)(2,1)S(1)}, bf16[1,192,384]{2,1,0:T(8,128)(2,1)S(1)}, u32[]{:S(2)}, u32[]{:S(2)}) collective-permute-start(bf16[1,192,384]{2,1,0:T(8,128)(2,1)S(1)} %get-tuple-element.12), channel_id=1, source_target_pairs={{0,2},{2,4},{4,6},{6,8},{8,10},{10,12},{12,14},{14,16},{16,18},{18... | collective-permute-start | bytes 442376 | tf_op jit(solution)/shard_map/ppermute | solution.py:24
  119.3 1.3 collective-permute-start.25
  120.6 3.0 %collective-permute-start.24 = (bf16[1,192,384]{2,1,0:T(8,128)(2,1)S(1)}, bf16[1,192,384]{2,1,0:T(8,128)(2,1)S(1)}, u32[]{:S(2)}, u32[]{:S(2)}) collective-permute-start(bf16[1,192,384]{2,1,0:T(8,128)(2,1)S(1)} %get-tuple-element.14), channel_id=1, source_target_pairs={{0,1},{2,3},{4,5},{6,7},{8,9},{10,11},{12,13},{14,15},{16,17},{18,... | collective-permute-start | bytes 442376 | tf_op jit(solution)/shard_map/ppermute | solution.py:24
  123.7 1.9 %collective-permute-start.23 = (bf16[1,192,384]{2,1,0:T(8,128)(2,1)S(1)}, bf16[1,192,384]{2,1,0:T(8,128)(2,1)S(1)}, u32[]{:S(2)}, u32[]{:S(2)}) collective-permute-start(bf16[1,192,384]{2,1,0:T(8,128)(2,1)S(1)} %get-tuple-element.15), channel_id=1, source_target_pairs={{2,0},{4,2},{6,4},{8,6},{10,8},{12,10},{14,12},{16,14},{18,16},{20... | collective-permute-start | bytes 442376 | tf_op jit(solution)/shard_map/ppermute | solution.py:27
  125.6 6.0 %collective-permute-done.23 = bf16[1,192,384]{2,1,0:T(8,128)(2,1)S(1)} collective-permute-done((bf16[1,192,384]{2,1,0:T(8,128)(2,1)S(1)}, bf16[1,192,384]{2,1,0:T(8,128)(2,1)S(1)}, u32[]{:S(2)}, u32[]{:S(2)}) %collective-permute-start.23) | collective-permute-done | bytes 147488 | tf_op jit(solution)/shard_map/ppermute | solution.py:27
  132.3 3.7 %collective-permute-start.26 = (bf16[1,192,384]{2,1,0:T(8,128)(2,1)S(1)}, bf16[1,192,384]{2,1,0:T(8,128)(2,1)S(1)}, u32[]{:S(2)}, u32[]{:S(2)}) collective-permute-start(bf16[1,192,384]{2,1,0:T(8,128)(2,1)S(1)} %get-tuple-element.8), channel_id=1, source_target_pairs={{0,2},{2,4},{4,6},{6,8},{8,10},{10,12},{12,14},{14,16},{16,18},{18... | collective-permute-start | bytes 442376 | tf_op jit(solution)/shard_map/ppermute | solution.py:24
  136.0 1.3 collective-permute-start.29
  137.3 3.0 %collective-permute-start.28 = (bf16[1,192,384]{2,1,0:T(8,128)(2,1)S(1)}, bf16[1,192,384]{2,1,0:T(8,128)(2,1)S(1)}, u32[]{:S(2)}, u32[]{:S(2)}) collective-permute-start(bf16[1,192,384]{2,1,0:T(8,128)(2,1)S(1)} %get-tuple-element.10), channel_id=1, source_target_pairs={{0,1},{2,3},{4,5},{6,7},{8,9},{10,11},{12,13},{14,15},{16,17},{18,... | collective-permute-start | bytes 442376 | tf_op jit(solution)/shard_map/ppermute | solution.py:24
  140.3 2.3 %collective-permute-start.27 = (bf16[1,192,384]{2,1,0:T(8,128)(2,1)S(1)}, bf16[1,192,384]{2,1,0:T(8,128)(2,1)S(1)}, u32[]{:S(2)}, u32[]{:S(2)}) collective-permute-start(bf16[1,192,384]{2,1,0:T(8,128)(2,1)S(1)} %get-tuple-element.11), channel_id=1, source_target_pairs={{2,0},{4,2},{6,4},{8,6},{10,8},{12,10},{14,12},{16,14},{18,16},{20... | collective-permute-start | bytes 442376 | tf_op jit(solution)/shard_map/ppermute | solution.py:27
  143.3 4.9 %collective-permute-done.27 = bf16[1,192,384]{2,1,0:T(8,128)(2,1)S(1)} collective-permute-done((bf16[1,192,384]{2,1,0:T(8,128)(2,1)S(1)}, bf16[1,192,384]{2,1,0:T(8,128)(2,1)S(1)}, u32[]{:S(2)}, u32[]{:S(2)}) %collective-permute-start.27) | collective-permute-done | bytes 147488 | tf_op jit(solution)/shard_map/ppermute | solution.py:27
  148.7 39.6 %all-reduce = (f32[192]{0:T(256)S(1)}, f32[192]{0:T(256)S(1)}) all-reduce(f32[192]{0:T(256)S(1)} %multiply_reduce_fusion.1, f32[192]{0:T(256)S(1)} %multiply_reduce_fusion), channel_id=1, replica_groups=mesh['gx'=16,'gy'=2] {'gx','gy'}, use_global_device_ids=true, to_apply=%region_1.3 | all-reduce | flops 384 | bytes 3072 | tf_op jit(solution)/shard_map/psum | solution.py:92
  188.2 2.3 %fusion.28 = bf16[1,1,4,192,384]{4,3,2,1,0:T(8,128)(2,1)} fusion(bf16[4,192,384]{2,1,0:T(8,128)(2,1)S(1)} %convolution_convert_fusion.1, bf16[4,192,384]{2,1,0:T(8,128)(2,1)S(1)} %convolution_convert_fusion.4, f32[192]{0:T(256)S(1)} %div.3, bf16[1,192,384]{2,1,0:T(8,128)(2,1)} %copy-done.20, bf16[1,192,384]{2,1,0:T(8,128)(2,1)} %copy-done.21, ...), kind=kLoop, calls=%fused_computation.44 | loop fusion | flops 4423680 | bytes 2949888 | tf_op jit(solution)/shard_map/broadcast_in_dim | solution.py:97
  (128 shorter events, 13.4 us)
Async XLA Ops:
  0.0 12.9 %copy-start = (bf16[1,1,4,384,384]{4,3,2,1,0:T(8,128)(2,1)S(1)}, bf16[1,1,4,384,384]{4,3,2,1,0:T(8,128)(2,1)}, u32[]{:S(2)}) copy-start(bf16[1,1,4,384,384]{4,3,2,1,0:T(8,128)(2,1)} %param.11) | copy-start | bytes 3538948
  0.0 12.9 %copy-start.2 = (bf16[1,1,4,192,384]{4,3,2,1,0:T(8,128)(2,1)S(1)}, bf16[1,1,4,192,384]{4,3,2,1,0:T(8,128)(2,1)}, u32[]{:S(2)}) copy-start(bf16[1,1,4,192,384]{4,3,2,1,0:T(8,128)(2,1)} %param.9) | copy-start | bytes 1769476
  1.3 10.2 %collective-permute-start = (bf16[1,192,384]{2,1,0:T(8,128)(2,1)S(1)}, bf16[1,192,384]{2,1,0:T(8,128)(2,1)S(1)}, u32[]{:S(2)}, u32[]{:S(2)}) collective-permute-start(bf16[1,192,384]{2,1,0:T(8,128)(2,1)S(1)} %get-tuple-element.24), channel_id=1, source_target_pairs={{0,2},{2,4},{4,6},{6,8},{8,10},{10,12},{12,14},{14,16},{16,18},{18... | collective-permute-start | bytes 442376 | tf_op jit(solution)/shard_map/ppermute | solution.py:24
  4.7 8.2 %collective-permute-start.1 = (bf16[1,192,384]{2,1,0:T(8,128)(2,1)S(1)}, bf16[1,192,384]{2,1,0:T(8,128)(2,1)S(1)}, u32[]{:S(2)}, u32[]{:S(2)}) collective-permute-start(bf16[1,192,384]{2,1,0:T(8,128)(2,1)S(1)} %get-tuple-element.25), channel_id=1, source_target_pairs={{2,0},{4,2},{6,4},{8,6},{10,8},{12,10},{14,12},{16,14},{18,16},{20... | collective-permute-start | bytes 442376 | tf_op jit(solution)/shard_map/ppermute | solution.py:27
  7.2 5.7 %collective-permute-start.3 = (bf16[1,192,384]{2,1,0:T(8,128)(2,1)S(1)}, bf16[1,192,384]{2,1,0:T(8,128)(2,1)S(1)}, u32[]{:S(2)}, u32[]{:S(2)}) collective-permute-start(bf16[1,192,384]{2,1,0:T(8,128)(2,1)S(1)} %get-tuple-element.26), channel_id=1, source_target_pairs={{1,0},{3,2},{5,4},{7,6},{9,8},{11,10},{13,12},{15,14},{17,16},{19,... | collective-permute-start | bytes 442376 | tf_op jit(solution)/shard_map/ppermute | solution.py:27
  8.5 4.5 %collective-permute-start.2 = (bf16[1,192,384]{2,1,0:T(8,128)(2,1)S(1)}, bf16[1,192,384]{2,1,0:T(8,128)(2,1)S(1)}, u32[]{:S(2)}, u32[]{:S(2)}) collective-permute-start(bf16[1,192,384]{2,1,0:T(8,128)(2,1)S(1)} %get-tuple-element.27), channel_id=1, source_target_pairs={{0,1},{2,3},{4,5},{6,7},{8,9},{10,11},{12,13},{14,15},{16,17},{18,... | collective-permute-start | bytes 442376 | tf_op jit(solution)/shard_map/ppermute | solution.py:24
  11.6 19.6 %copy-start.39 = (s32[1,1,4]{2,1,0:T(1,128)S(1)}, s32[1,1,4]{2,1,0:T(1,128)}, u32[]{:S(2)}) copy-start(s32[1,1,4]{2,1,0:T(1,128)} %param.15) | copy-start | bytes 52
  13.0 27.9 %copy-start.1 = (bf16[1,1,4,384,384]{4,3,2,1,0:T(8,128)(2,1)S(1)}, bf16[1,1,4,384,384]{4,3,2,1,0:T(8,128)(2,1)}, u32[]{:S(2)}) copy-start(bf16[1,1,4,384,384]{4,3,2,1,0:T(8,128)(2,1)} %param.12) | copy-start | bytes 3538948
  14.0 3.1 %collective-permute-start.4 = (bf16[4,192]{1,0:T(4,128)(2,1)S(1)}, bf16[4,192]{1,0:T(4,128)(2,1)S(1)}, u32[]{:S(2)}, u32[]{:S(2)}) collective-permute-start(bf16[4,192]{1,0:T(4,128)(2,1)S(1)} %fusion.22), channel_id=1, source_target_pairs={{0,31},{1,0},{2,1},{3,2},{4,3},{5,4},{6,5},{7,6},{8,7},{9,8},{10,9... | collective-permute-start | bytes 4616 | tf_op jit(solution)/shard_map/ppermute | solution.py:12
  17.1 4.6 %collective-permute-start.5 = (bf16[8,192]{1,0:T(8,128)(2,1)S(1)}, bf16[8,192]{1,0:T(8,128)(2,1)S(1)}, u32[]{:S(2)}, u32[]{:S(2)}) collective-permute-start(bf16[8,192]{1,0:T(8,128)(2,1)S(1)} %pad_maximum_fusion.9), channel_id=1, source_target_pairs={{0,30},{1,31},{2,0},{3,1},{4,2},{5,3},{6,4},{7,5},{8,6},{9,7},{10,... | collective-permute-start | bytes 9224 | tf_op jit(solution)/shard_map/ppermute | solution.py:12
  21.7 3.7 %collective-permute-start.6 = (bf16[16,192]{1,0:T(8,128)(2,1)S(1)}, bf16[16,192]{1,0:T(8,128)(2,1)S(1)}, u32[]{:S(2)}, u32[]{:S(2)}) collective-permute-start(bf16[16,192]{1,0:T(8,128)(2,1)S(1)} %pad_maximum_fusion.7), channel_id=1, source_target_pairs={{0,28},{1,29},{2,30},{3,31},{4,0},{5,1},{6,2},{7,3},{8,4},{9,5},{1... | collective-permute-start | bytes 18440 | tf_op jit(solution)/shard_map/ppermute | solution.py:12
  26.6 6.2 %collective-permute-start.7 = (bf16[32,192]{1,0:T(8,128)(2,1)}, bf16[32,192]{1,0:T(8,128)(2,1)}, u32[]{:S(2)}, u32[]{:S(2)}) collective-permute-start(bf16[32,192]{1,0:T(8,128)(2,1)} %pad_maximum_fusion.5), channel_id=1, source_target_pairs={{0,24},{1,25},{2,26},{3,27},{4,28},{5,29},{6,30},{7,31},{8,0},{9,1... | collective-permute-start | bytes 36872 | tf_op jit(solution)/shard_map/ppermute | solution.py:12
  37.3 5.8 %collective-permute-start.8 = (bf16[64,192]{1,0:T(8,128)(2,1)}, bf16[64,192]{1,0:T(8,128)(2,1)}, u32[]{:S(2)}, u32[]{:S(2)}) collective-permute-start(bf16[64,192]{1,0:T(8,128)(2,1)} %concatenate.44), channel_id=1, source_target_pairs={{0,16},{1,17},{2,18},{3,19},{4,20},{5,21},{6,22},{7,23},{8,24},{9,... | collective-permute-start | bytes 73736 | tf_op jit(solution)/shard_map/ppermute | solution.py:12
  52.2 18.2 %copy-start.37 = (bf16[1,1,4,384,384]{4,3,2,1,0:T(8,128)(2,1)S(1)}, bf16[1,1,4,384,384]{4,3,2,1,0:T(8,128)(2,1)}, u32[]{:S(2)}) copy-start(bf16[1,1,4,384,384]{4,3,2,1,0:T(8,128)(2,1)} %param.10) | copy-start | bytes 3538948
  52.3 10.3 %collective-permute-start.9 = (bf16[1,192,384]{2,1,0:T(8,128)(2,1)S(1)}, bf16[1,192,384]{2,1,0:T(8,128)(2,1)S(1)}, u32[]{:S(2)}, u32[]{:S(2)}) collective-permute-start(bf16[1,192,384]{2,1,0:T(8,128)(2,1)S(1)} %get-tuple-element.20), channel_id=1, source_target_pairs={{0,2},{2,4},{4,6},{6,8},{8,10},{10,12},{12,14},{14,16},{16,18},{18... | collective-permute-start | bytes 442376 | tf_op jit(solution)/shard_map/ppermute | solution.py:24
  55.7 7.0 %collective-permute-start.12 = (bf16[1,192,384]{2,1,0:T(8,128)(2,1)S(1)}, bf16[1,192,384]{2,1,0:T(8,128)(2,1)S(1)}, u32[]{:S(2)}, u32[]{:S(2)}) collective-permute-start(bf16[1,192,384]{2,1,0:T(8,128)(2,1)S(1)} %get-tuple-element.21), channel_id=1, source_target_pairs={{1,0},{3,2},{5,4},{7,6},{9,8},{11,10},{13,12},{15,14},{17,16},{19,... | collective-permute-start | bytes 442376 | tf_op jit(solution)/shard_map/ppermute | solution.py:27
  57.0 5.7 %collective-permute-start.11 = (bf16[1,192,384]{2,1,0:T(8,128)(2,1)S(1)}, bf16[1,192,384]{2,1,0:T(8,128)(2,1)S(1)}, u32[]{:S(2)}, u32[]{:S(2)}) collective-permute-start(bf16[1,192,384]{2,1,0:T(8,128)(2,1)S(1)} %get-tuple-element.22), channel_id=1, source_target_pairs={{0,1},{2,3},{4,5},{6,7},{8,9},{10,11},{12,13},{14,15},{16,17},{18,... | collective-permute-start | bytes 442376 | tf_op jit(solution)/shard_map/ppermute | solution.py:24
  60.0 10.4 %collective-permute-start.10 = (bf16[1,192,384]{2,1,0:T(8,128)(2,1)S(1)}, bf16[1,192,384]{2,1,0:T(8,128)(2,1)S(1)}, u32[]{:S(2)}, u32[]{:S(2)}) collective-permute-start(bf16[1,192,384]{2,1,0:T(8,128)(2,1)S(1)} %get-tuple-element.23), channel_id=1, source_target_pairs={{2,0},{4,2},{6,4},{8,6},{10,8},{12,10},{14,12},{16,14},{18,16},{20... | collective-permute-start | bytes 442376 | tf_op jit(solution)/shard_map/ppermute | solution.py:27
  71.1 16.9 %copy-start.4 = (bf16[4,192,384]{2,1,0:T(8,128)(2,1)}, bf16[4,192,384]{2,1,0:T(8,128)(2,1)S(1)}, u32[]{:S(2)}) copy-start(bf16[4,192,384]{2,1,0:T(8,128)(2,1)S(1)} %convolution_convert_fusion.3) | copy-start | bytes 1769476
  71.1 16.2 %copy-start.8 = (bf16[1,192,384]{2,1,0:T(8,128)(2,1)S(1)}, bf16[1,192,384]{2,1,0:T(8,128)(2,1)}, u32[]{:S(2)}) copy-start(bf16[1,192,384]{2,1,0:T(8,128)(2,1)} %copy-done.7) | copy-start | bytes 442372
  71.1 16.2 %copy-start.11 = (bf16[1,192,384]{2,1,0:T(8,128)(2,1)S(1)}, bf16[1,192,384]{2,1,0:T(8,128)(2,1)}, u32[]{:S(2)}) copy-start(bf16[1,192,384]{2,1,0:T(8,128)(2,1)} %copy-done.10) | copy-start | bytes 442372
  71.1 16.2 %copy-start.14 = (bf16[1,192,384]{2,1,0:T(8,128)(2,1)S(1)}, bf16[1,192,384]{2,1,0:T(8,128)(2,1)}, u32[]{:S(2)}) copy-start(bf16[1,192,384]{2,1,0:T(8,128)(2,1)} %copy-done.13) | copy-start | bytes 442372
  71.1 16.2 %copy-start.17 = (bf16[1,192,384]{2,1,0:T(8,128)(2,1)S(1)}, bf16[1,192,384]{2,1,0:T(8,128)(2,1)}, u32[]{:S(2)}) copy-start(bf16[1,192,384]{2,1,0:T(8,128)(2,1)} %copy-done.16) | copy-start | bytes 442372
  71.2 10.4 %collective-permute-start.13 = (bf16[1,192,384]{2,1,0:T(8,128)(2,1)S(1)}, bf16[1,192,384]{2,1,0:T(8,128)(2,1)S(1)}, u32[]{:S(2)}, u32[]{:S(2)}) collective-permute-start(bf16[1,192,384]{2,1,0:T(8,128)(2,1)S(1)} %get-tuple-element.16), channel_id=1, source_target_pairs={{0,2},{2,4},{4,6},{6,8},{8,10},{10,12},{12,14},{14,16},{16,18},{18... | collective-permute-start | bytes 442376 | tf_op jit(solution)/shard_map/ppermute | solution.py:24
  75.0 6.6 %collective-permute-start.16 = (bf16[1,192,384]{2,1,0:T(8,128)(2,1)S(1)}, bf16[1,192,384]{2,1,0:T(8,128)(2,1)S(1)}, u32[]{:S(2)}, u32[]{:S(2)}) collective-permute-start(bf16[1,192,384]{2,1,0:T(8,128)(2,1)S(1)} %get-tuple-element.17), channel_id=1, source_target_pairs={{1,0},{3,2},{5,4},{7,6},{9,8},{11,10},{13,12},{15,14},{17,16},{19,... | collective-permute-start | bytes 442376 | tf_op jit(solution)/shard_map/ppermute | solution.py:27
  76.3 5.3 %collective-permute-start.15 = (bf16[1,192,384]{2,1,0:T(8,128)(2,1)S(1)}, bf16[1,192,384]{2,1,0:T(8,128)(2,1)S(1)}, u32[]{:S(2)}, u32[]{:S(2)}) collective-permute-start(bf16[1,192,384]{2,1,0:T(8,128)(2,1)S(1)} %get-tuple-element.18), channel_id=1, source_target_pairs={{0,1},{2,3},{4,5},{6,7},{8,9},{10,11},{12,13},{14,15},{16,17},{18,... | collective-permute-start | bytes 442376 | tf_op jit(solution)/shard_map/ppermute | solution.py:24
  79.3 7.9 %collective-permute-start.14 = (bf16[1,192,384]{2,1,0:T(8,128)(2,1)S(1)}, bf16[1,192,384]{2,1,0:T(8,128)(2,1)S(1)}, u32[]{:S(2)}, u32[]{:S(2)}) collective-permute-start(bf16[1,192,384]{2,1,0:T(8,128)(2,1)S(1)} %get-tuple-element.19), channel_id=1, source_target_pairs={{2,0},{4,2},{6,4},{8,6},{10,8},{12,10},{14,12},{16,14},{18,16},{20... | collective-permute-start | bytes 442376 | tf_op jit(solution)/shard_map/ppermute | solution.py:27
  88.8 1.3 collective-permute-start.17
  90.2 4.6 %collective-permute-start.18 = (bf16[8,192]{1,0:T(8,128)(2,1)S(1)}, bf16[8,192]{1,0:T(8,128)(2,1)S(1)}, u32[]{:S(2)}, u32[]{:S(2)}) collective-permute-start(bf16[8,192]{1,0:T(8,128)(2,1)S(1)} %pad_maximum_fusion.10), channel_id=1, source_target_pairs={{0,30},{1,31},{2,0},{3,1},{4,2},{5,3},{6,4},{7,5},{8,6},{9,7},{10,... | collective-permute-start | bytes 9224 | tf_op jit(solution)/shard_map/ppermute | solution.py:12
  94.8 3.8 %collective-permute-start.19 = (bf16[16,192]{1,0:T(8,128)(2,1)S(1)}, bf16[16,192]{1,0:T(8,128)(2,1)S(1)}, u32[]{:S(2)}, u32[]{:S(2)}) collective-permute-start(bf16[16,192]{1,0:T(8,128)(2,1)S(1)} %pad_maximum_fusion.8), channel_id=1, source_target_pairs={{0,28},{1,29},{2,30},{3,31},{4,0},{5,1},{6,2},{7,3},{8,4},{9,5},{1... | collective-permute-start | bytes 18440 | tf_op jit(solution)/shard_map/ppermute | solution.py:12
  98.6 3.8 %collective-permute-start.20 = (bf16[32,192]{1,0:T(8,128)(2,1)S(1)}, bf16[32,192]{1,0:T(8,128)(2,1)S(1)}, u32[]{:S(2)}, u32[]{:S(2)}) collective-permute-start(bf16[32,192]{1,0:T(8,128)(2,1)S(1)} %pad_maximum_fusion.6), channel_id=1, source_target_pairs={{0,24},{1,25},{2,26},{3,27},{4,28},{5,29},{6,30},{7,31},{8,0},{9,1... | collective-permute-start | bytes 36872 | tf_op jit(solution)/shard_map/ppermute | solution.py:12
  102.4 7.2 %collective-permute-start.21 = (bf16[64,192]{1,0:T(8,128)(2,1)S(1)}, bf16[64,192]{1,0:T(8,128)(2,1)S(1)}, u32[]{:S(2)}, u32[]{:S(2)}) collective-permute-start(bf16[64,192]{1,0:T(8,128)(2,1)S(1)} %concatenate.49), channel_id=1, source_target_pairs={{0,16},{1,17},{2,18},{3,19},{4,20},{5,21},{6,22},{7,23},{8,24},{9,... | collective-permute-start | bytes 73736 | tf_op jit(solution)/shard_map/ppermute | solution.py:12
  114.6 17.0 %copy-start.38 = (bf16[1,1,4,384,384]{4,3,2,1,0:T(8,128)(2,1)S(1)}, bf16[1,1,4,384,384]{4,3,2,1,0:T(8,128)(2,1)}, u32[]{:S(2)}) copy-start(bf16[1,1,4,384,384]{4,3,2,1,0:T(8,128)(2,1)} %param.10) | copy-start | bytes 3538948
  114.7 10.9 %collective-permute-start.22 = (bf16[1,192,384]{2,1,0:T(8,128)(2,1)S(1)}, bf16[1,192,384]{2,1,0:T(8,128)(2,1)S(1)}, u32[]{:S(2)}, u32[]{:S(2)}) collective-permute-start(bf16[1,192,384]{2,1,0:T(8,128)(2,1)S(1)} %get-tuple-element.12), channel_id=1, source_target_pairs={{0,2},{2,4},{4,6},{6,8},{8,10},{10,12},{12,14},{14,16},{16,18},{18... | collective-permute-start | bytes 442376 | tf_op jit(solution)/shard_map/ppermute | solution.py:24
  119.3 6.3 %collective-permute-start.25 = (bf16[1,192,384]{2,1,0:T(8,128)(2,1)S(1)}, bf16[1,192,384]{2,1,0:T(8,128)(2,1)S(1)}, u32[]{:S(2)}, u32[]{:S(2)}) collective-permute-start(bf16[1,192,384]{2,1,0:T(8,128)(2,1)S(1)} %get-tuple-element.13), channel_id=1, source_target_pairs={{1,0},{3,2},{5,4},{7,6},{9,8},{11,10},{13,12},{15,14},{17,16},{19,... | collective-permute-start | bytes 442376 | tf_op jit(solution)/shard_map/ppermute | solution.py:27
  120.6 5.0 %collective-permute-start.24 = (bf16[1,192,384]{2,1,0:T(8,128)(2,1)S(1)}, bf16[1,192,384]{2,1,0:T(8,128)(2,1)S(1)}, u32[]{:S(2)}, u32[]{:S(2)}) collective-permute-start(bf16[1,192,384]{2,1,0:T(8,128)(2,1)S(1)} %get-tuple-element.14), channel_id=1, source_target_pairs={{0,1},{2,3},{4,5},{6,7},{8,9},{10,11},{12,13},{14,15},{16,17},{18,... | collective-permute-start | bytes 442376 | tf_op jit(solution)/shard_map/ppermute | solution.py:24
  123.7 7.9 %collective-permute-start.23 = (bf16[1,192,384]{2,1,0:T(8,128)(2,1)S(1)}, bf16[1,192,384]{2,1,0:T(8,128)(2,1)S(1)}, u32[]{:S(2)}, u32[]{:S(2)}) collective-permute-start(bf16[1,192,384]{2,1,0:T(8,128)(2,1)S(1)} %get-tuple-element.15), channel_id=1, source_target_pairs={{2,0},{4,2},{6,4},{8,6},{10,8},{12,10},{14,12},{16,14},{18,16},{20... | collective-permute-start | bytes 442376 | tf_op jit(solution)/shard_map/ppermute | solution.py:27
  131.6 11.0 %copy-start.12 = (bf16[1,192,384]{2,1,0:T(8,128)(2,1)S(1)}, bf16[1,192,384]{2,1,0:T(8,128)(2,1)}, u32[]{:S(2)}) copy-start(bf16[1,192,384]{2,1,0:T(8,128)(2,1)} %copy-done.10) | copy-start | bytes 442372
  131.6 11.0 %copy-start.15 = (bf16[1,192,384]{2,1,0:T(8,128)(2,1)S(1)}, bf16[1,192,384]{2,1,0:T(8,128)(2,1)}, u32[]{:S(2)}) copy-start(bf16[1,192,384]{2,1,0:T(8,128)(2,1)} %copy-done.13) | copy-start | bytes 442372
  131.6 11.1 %copy-start.18 = (bf16[1,192,384]{2,1,0:T(8,128)(2,1)S(1)}, bf16[1,192,384]{2,1,0:T(8,128)(2,1)}, u32[]{:S(2)}) copy-start(bf16[1,192,384]{2,1,0:T(8,128)(2,1)} %copy-done.16) | copy-start | bytes 442372
  131.6 11.1 %copy-start.24 = (bf16[1,192,384]{2,1,0:T(8,128)(2,1)S(1)}, bf16[1,192,384]{2,1,0:T(8,128)(2,1)}, u32[]{:S(2)}) copy-start(bf16[1,192,384]{2,1,0:T(8,128)(2,1)} %copy-done.23) | copy-start | bytes 442372
  131.6 11.1 %copy-start.26 = (bf16[1,192,384]{2,1,0:T(8,128)(2,1)S(1)}, bf16[1,192,384]{2,1,0:T(8,128)(2,1)}, u32[]{:S(2)}) copy-start(bf16[1,192,384]{2,1,0:T(8,128)(2,1)} %copy-done.25) | copy-start | bytes 442372
  131.6 11.1 %copy-start.28 = (bf16[1,192,384]{2,1,0:T(8,128)(2,1)S(1)}, bf16[1,192,384]{2,1,0:T(8,128)(2,1)}, u32[]{:S(2)}) copy-start(bf16[1,192,384]{2,1,0:T(8,128)(2,1)} %copy-done.27) | copy-start | bytes 442372
  131.7 11.1 %copy-start.30 = (bf16[1,192,384]{2,1,0:T(8,128)(2,1)S(1)}, bf16[1,192,384]{2,1,0:T(8,128)(2,1)}, u32[]{:S(2)}) copy-start(bf16[1,192,384]{2,1,0:T(8,128)(2,1)} %copy-done.29) | copy-start | bytes 442372
  132.3 11.0 %collective-permute-start.26 = (bf16[1,192,384]{2,1,0:T(8,128)(2,1)S(1)}, bf16[1,192,384]{2,1,0:T(8,128)(2,1)S(1)}, u32[]{:S(2)}, u32[]{:S(2)}) collective-permute-start(bf16[1,192,384]{2,1,0:T(8,128)(2,1)S(1)} %get-tuple-element.8), channel_id=1, source_target_pairs={{0,2},{2,4},{4,6},{6,8},{8,10},{10,12},{12,14},{14,16},{16,18},{18... | collective-permute-start | bytes 442376 | tf_op jit(solution)/shard_map/ppermute | solution.py:24
  136.0 7.3 %collective-permute-start.29 = (bf16[1,192,384]{2,1,0:T(8,128)(2,1)S(1)}, bf16[1,192,384]{2,1,0:T(8,128)(2,1)S(1)}, u32[]{:S(2)}, u32[]{:S(2)}) collective-permute-start(bf16[1,192,384]{2,1,0:T(8,128)(2,1)S(1)} %get-tuple-element.9), channel_id=1, source_target_pairs={{1,0},{3,2},{5,4},{7,6},{9,8},{11,10},{13,12},{15,14},{17,16},{19,... | collective-permute-start | bytes 442376 | tf_op jit(solution)/shard_map/ppermute | solution.py:27
  137.3 6.0 %collective-permute-start.28 = (bf16[1,192,384]{2,1,0:T(8,128)(2,1)S(1)}, bf16[1,192,384]{2,1,0:T(8,128)(2,1)S(1)}, u32[]{:S(2)}, u32[]{:S(2)}) collective-permute-start(bf16[1,192,384]{2,1,0:T(8,128)(2,1)S(1)} %get-tuple-element.10), channel_id=1, source_target_pairs={{0,1},{2,3},{4,5},{6,7},{8,9},{10,11},{12,13},{14,15},{16,17},{18,... | collective-permute-start | bytes 442376 | tf_op jit(solution)/shard_map/ppermute | solution.py:24
  140.3 7.9 %collective-permute-start.27 = (bf16[1,192,384]{2,1,0:T(8,128)(2,1)S(1)}, bf16[1,192,384]{2,1,0:T(8,128)(2,1)S(1)}, u32[]{:S(2)}, u32[]{:S(2)}) collective-permute-start(bf16[1,192,384]{2,1,0:T(8,128)(2,1)S(1)} %get-tuple-element.11), channel_id=1, source_target_pairs={{2,0},{4,2},{6,4},{8,6},{10,8},{12,10},{14,12},{16,14},{18,16},{20... | collective-permute-start | bytes 442376 | tf_op jit(solution)/shard_map/ppermute | solution.py:27
  (22 other events, 112.7 us)
